TPU v7x, 512 devices: a whole 4x4x16 slice. The times are simulated.
512 devices in a mesh: scen: 16 (over x, z_hi), graph: 32 (over y, z_lo, core).
Axes of the slice: x: 4, y: 4, z: 16 (z_hi: 4, z_lo: 4; z = z_hi * 4 + z_lo), core: 2. Of those that a mesh axis runs over, the one named last changes fastest.
Arguments:
- features: bfloat16 [32, 8192, 256], P('scen', 'graph'), may hold values from -6 to 6
- cotangent: bfloat16 [32, 8192, 256], P('scen', 'graph'), may hold values from -6 to 6
- adjacency_tiles: bfloat16 [32, 2, 4, 128, 128], P('graph'), may hold values from -0.25 to 0.25
- tile_columns: int32 [32, 2, 4], P('graph'), may hold values from 0 to 5, as said below
- boundary: int32 [32, 4, 128], P('graph'), may hold values from 0 to 255, as said below
- self_weight1: bfloat16 [256, 256], replicated, may hold values from -0.375 to 0.375
- message_weight1: bfloat16 [256, 256], replicated, may hold values from -0.375 to 0.375
- self_weight2: bfloat16 [256, 256], replicated, may hold values from -0.375 to 0.375
- message_weight2: bfloat16 [256, 256], replicated, may hold values from -0.375 to 0.375
Outputs:
- input_grad: bfloat16 [32, 8192, 256], P('scen', 'graph')
- self_grad1: float32 [256, 256], P('graph')
- message_grad1: float32 [256, 256], P('graph')
- self_grad2: float32 [256, 256], P('graph')
- message_grad2: float32 [256, 256], P('graph')
Inputs may be any that keep to these rules, and one draw needn't show every extreme that they name: `tile_columns`: in tile row r of every partition, tile 0 has column r, tiles 1 and 2 name halo columns (2 or more), tile 3 a local column other than r; every one of the 4 halo columns is named in every partition. `boundary`: each list names 128 distinct local rows and holds rows 0 and 255.
All inputs are finite; a program needn't handle non-finite values.
Results may differ from a plain program's by a relative error of at most 0.015.
Values may be sent and summed in bfloat16 or wider, within the bound.
No kernel may reach another device: no remote copies, remote signals or barrier semaphores. Data moves between devices by JAX's collectives and lax.ppermute only.
A program may use at most 64 MiB of HBM per device.

v0:
```python
import math

import jax
import jax.numpy as jnp
from jax import lax
from jax.sharding import PartitionSpec as P

shift_offsets = (1, 2, -1, -2)


def from_behind(value, axis, steps):
    count = lax.axis_size(axis)
    first, last = (max(0, -steps), min(count, count - steps))
    return lax.ppermute(value, axis, [(source, source + steps) for source in range(first, last)])


def silu_grad(values):
    sigma = jax.nn.sigmoid(values)
    return sigma * (1.0 + values * (1.0 - sigma))


def pass_blocks(slots, sign):
    received = [
        from_behind(slots[number], "graph", sign * shift_offsets[number]) for number in range(4)
    ]
    return received


def weight_sums(layer_input_rows, neighbor_message, preactivation_gradient):
    width = layer_input_rows.shape[-1]
    flat_in = layer_input_rows.reshape(-1, width)
    flat_message = neighbor_message.reshape(-1, width)
    flat_grad = preactivation_gradient.reshape(-1, width)
    contract = (((0,), (0,)), ((), ()))
    share_rows = width // lax.axis_size("graph")
    stacked = jnp.stack(
        (
            lax.dot_general(flat_in, flat_grad, contract, preferred_element_type=jnp.float32),
            lax.dot_general(flat_message, flat_grad, contract, preferred_element_type=jnp.float32),
        ),
        1,
    )
    total = lax.psum(stacked, ("scen", "graph"))
    share = lax.dynamic_slice_in_dim(total, lax.axis_index("graph") * share_rows, share_rows, 0)
    total_rows = flat_in.shape[0] * lax.axis_size("scen") * lax.axis_size("graph")
    scale = 1.0 / math.sqrt(total_rows)
    return (share[:, 0] * scale, share[:, 1] * scale)


def forward(layer_input_rows, self_matrix, message_matrix, adjacency, columns, boundary):
    scen_count, bus_count, width = layer_input_rows.shape
    block_rows = adjacency.shape[-1]
    slots = [layer_input_rows[:, boundary[number], :] for number in range(4)]
    received = pass_blocks(slots, 1)
    extended = jnp.concatenate([layer_input_rows] + received, axis=1)
    tile_blocks = extended.reshape(scen_count, -1, block_rows, width)
    picked = tile_blocks[:, columns]
    neighbor_message = jnp.einsum(
        "rjab,srjbd->srad", adjacency, picked, preferred_element_type=jnp.float32
    )
    neighbor_message = neighbor_message.reshape(scen_count, bus_count, width).astype(jnp.bfloat16)
    preactivation = jnp.einsum(
        "oyp,pw->oyw", layer_input_rows, self_matrix, preferred_element_type=jnp.float32
    )
    preactivation = preactivation + jnp.einsum(
        "oyp,pw->oyw", neighbor_message, message_matrix, preferred_element_type=jnp.float32
    )
    return (neighbor_message, preactivation)


def backward(
    layer_input_rows,
    neighbor_message,
    preactivation,
    out_grad,
    self_matrix,
    message_matrix,
    adjacency,
    columns,
    boundary,
):
    scen_count, bus_count, width = layer_input_rows.shape
    block_rows = adjacency.shape[-1]
    tile_rows = columns.shape[0]
    preactivation_gradient = (out_grad.astype(jnp.float32) * silu_grad(preactivation)).astype(
        jnp.bfloat16
    )
    grads = weight_sums(layer_input_rows, neighbor_message, preactivation_gradient)
    self_contribution = jnp.einsum(
        "lqf,af->lqa", preactivation_gradient, self_matrix, preferred_element_type=jnp.float32
    )
    message_grad = jnp.einsum(
        "lqf,af->lqa", preactivation_gradient, message_matrix, preferred_element_type=jnp.float32
    )
    message_grad = message_grad.astype(jnp.bfloat16).reshape(
        scen_count, tile_rows, block_rows, width
    )
    spread = jnp.einsum(
        "rjab,srad->srjbd", adjacency, message_grad, preferred_element_type=jnp.float32
    )
    column_count = tile_rows + 4
    onehot = (
        columns[:, :, None] == jnp.arange(column_count, dtype=jnp.int32)[None, None, :]
    ).astype(jnp.float32)
    tile_grad = jnp.einsum("rjc,srjbd->scbd", onehot, spread, precision=lax.Precision.HIGHEST)
    accum = self_contribution + tile_grad[:, :tile_rows].reshape(scen_count, bus_count, width)
    halo_grad = tile_grad[:, tile_rows:].astype(jnp.bfloat16)
    returned = pass_blocks([halo_grad[:, number] for number in range(4)], -1)
    for number in range(4):
        accum = accum.at[:, boundary[number], :].add(returned[number].astype(jnp.float32))
    return (accum.astype(jnp.bfloat16), grads)


def local(
    features,
    cotangent,
    adjacency_tiles,
    tile_columns,
    boundary,
    self_weight1,
    message_weight1,
    self_weight2,
    message_weight2,
):
    adjacency = adjacency_tiles[0]
    columns = tile_columns[0]
    row_lists = boundary[0]
    message1, pre1 = forward(features, self_weight1, message_weight1, adjacency, columns, row_lists)
    hidden = jax.nn.silu(pre1).astype(jnp.bfloat16)
    message2, pre2 = forward(hidden, self_weight2, message_weight2, adjacency, columns, row_lists)
    hidden_grad, grads2 = backward(
        hidden,
        message2,
        pre2,
        cotangent,
        self_weight2,
        message_weight2,
        adjacency,
        columns,
        row_lists,
    )
    input_grad, grads1 = backward(
        features,
        message1,
        pre1,
        hidden_grad,
        self_weight1,
        message_weight1,
        adjacency,
        columns,
        row_lists,
    )
    return (input_grad, grads1[0], grads1[1], grads2[0], grads2[1])


def solution(mesh):
    in_specs = (
        P("scen", "graph", None),
        P("scen", "graph", None),
        P("graph", None, None, None, None),
        P("graph", None, None),
        P("graph", None, None),
        P(),
        P(),
        P(),
        P(),
    )
    out_specs = (
        P("scen", "graph", None),
        P("graph", None),
        P("graph", None),
        P("graph", None),
        P("graph", None),
    )
    return jax.shard_map(local, mesh=mesh, in_specs=in_specs, out_specs=out_specs, check_vma=False)
```

profile of v0, /device:TPU:1, one launch (start us, length us, event | category | flops | bytes accessed | tf_op | source)
XLA Modules:
  0.0 624.8 jit_solution(15803925400027915507)
XLA Ops:
  8.6 2.0 gather_fusion
  10.7 4.9 collective-permute-start
  15.6 2.0 gather_fusion.1
  17.6 3.5 collective-permute-start.1
  22.3 2.9 collective-permute-start.2
  28.6 4.8 collective-permute-done.3
  38.3 3.2 collective-permute-start.4
  41.5 2.8 collective-permute-start.5
  47.4 1.9 collective-permute-start.6
  50.7 3.0 collective-permute-done.6
  53.7 3.3 collective-permute-done.7
  60.4 1.8 fusion.16
  62.2 2.3 copy.80
  64.5 1.6 fusion.47
  67.6 2.1 collective-permute-start.8
  71.7 5.9 collective-permute-start.10
  77.6 3.8 collective-permute-start.11
  84.2 5.2 scatter_fusion
  89.3 5.2 scatter_fusion.1
  94.5 5.2 scatter_fusion.2
  99.7 5.2 scatter_fusion.3
  107.3 1.8 fusion.18
  109.1 2.3 copy.84
  111.4 1.6 fusion.48
  115.1 2.1 collective-permute-start.12
  119.2 4.4 collective-permute-start.14
  123.6 4.1 collective-permute-start.15
  130.3 5.2 scatter_fusion.4
  135.4 5.2 scatter_fusion.5
  140.6 5.2 scatter_fusion.6
  145.8 5.2 scatter_fusion.7
  151.9 461.3 %all-reduce.3.cloned.1.call-done = (f32[256,2,256]{0,2,1:T(8,128)}, f32[256,2,256]{0,2,1:T(8,128)}) async-done(((f32[256,2,256]{0,2,1:T(8,128)}, f32[256,2,256]{0,2,1:T(8,128)}), (f32[256,2,256]{0,2,1:T(8,128)}, f32[256,2,256]{0,2,1:T(8,128)})) %all-reduce.3.cloned.1.call-update) | async-done | bytes 1048592 | tf_op jit(solution)/shard_map/psum | solution.py:43
  (148 shorter events, 39.3 us)
Async XLA Ops:
  7.2 26.9 %copy-start = (bf16[1,2,4,128,128]{4,3,2,1,0:T(8,128)(2,1)S(1)}, bf16[1,2,4,128,128]{4,3,2,1,0:T(8,128)(2,1)}, u32[]{:S(2)}) copy-start(bf16[1,2,4,128,128]{4,3,2,1,0:T(8,128)(2,1)} %param.11) | copy-start | bytes 786436
  7.2 14.1 %copy-start.1 = (bf16[2,256,256]{2,1,0:T(8,128)(2,1)S(1)}, bf16[2,256,256]{2,1,0:T(8,128)(2,1)}, u32[]{:S(2)}) copy-start(bf16[2,256,256]{2,1,0:T(8,128)(2,1)} %param.9) | copy-start | bytes 786436
  7.2 605.9 %all-reduce.3.cloned.1.call-start = ((), (), s32[]{:S(2)}) async-start(), calls=%async_computation | async-start | bytes 2097152 | tf_op jit(solution)/shard_map/psum | solution.py:43
  8.6 7.0 %copy-start.19 = (s32[1024]{0:T(1024)}, s32[1024]{0:T(1024)S(1)}, u32[]{:S(2)}) copy-start(s32[1024]{0:T(1024)S(1)} %get-tuple-element.43) | copy-start | bytes 12292
  8.6 12.6 %copy-start.18 = (s32[1024]{0:T(1024)}, s32[1024]{0:T(1024)S(1)}, u32[]{:S(2)}) copy-start(s32[1024]{0:T(1024)S(1)} %get-tuple-element.42) | copy-start | bytes 12292
  8.6 19.0 %copy-start.6 = (bf16[256,256]{1,0:T(8,128)(2,1)S(1)}, bf16[256,256]{1,0:T(8,128)(2,1)}, u32[]{:S(2)}) copy-start(bf16[256,256]{1,0:T(8,128)(2,1)} %param.14) | copy-start | bytes 393220
  10.7 17.3 %collective-permute-start = (bf16[2,128,256]{2,1,0:T(8,128)(2,1)S(1)}, bf16[2,128,256]{2,1,0:T(8,128)(2,1)S(1)}, u32[]{:S(2)}, u32[]{:S(2)}) collective-permute-start(bf16[2,128,256]{2,1,0:T(8,128)(2,1)S(1)} %bitcast.242), channel_id=1, source_target_pairs={{0,1},{1,2},{2,3},{3,4},{4,5},{5,6},{6,7},{7,8},{8,9},{9,10},{10,1... | collective-permute-start | bytes 393224 | tf_op jit(solution)/shard_map/ppermute | solution.py:14
  15.6 12.2 %copy-start.11 = (s32[1,2,4]{2,1,0:T(2,128)S(1)}, s32[1,2,4]{2,1,0:T(2,128)}, u32[]{:S(2)}) copy-start(s32[1,2,4]{2,1,0:T(2,128)} %param.12) | copy-start | bytes 100
  17.6 10.4 %collective-permute-start.1 = (bf16[2,128,256]{2,1,0:T(8,128)(2,1)S(1)}, bf16[2,128,256]{2,1,0:T(8,128)(2,1)S(1)}, u32[]{:S(2)}, u32[]{:S(2)}) collective-permute-start(bf16[2,128,256]{2,1,0:T(8,128)(2,1)S(1)} %bitcast.241), channel_id=1, source_target_pairs={{0,2},{1,3},{2,4},{3,5},{4,6},{5,7},{6,8},{7,9},{8,10},{9,11},{10,... | collective-permute-start | bytes 393224 | tf_op jit(solution)/shard_map/ppermute | solution.py:14
  21.2 4.0 copy-start.17
  21.2 6.8 %copy-start.16 = (s32[1024]{0:T(1024)}, s32[1024]{0:T(1024)S(1)}, u32[]{:S(2)}) copy-start(s32[1024]{0:T(1024)S(1)} %get-tuple-element.40) | copy-start | bytes 12292
  22.3 6.3 %collective-permute-start.2 = (bf16[2,128,256]{2,1,0:T(8,128)(2,1)S(1)}, bf16[2,128,256]{2,1,0:T(8,128)(2,1)S(1)}, u32[]{:S(2)}, u32[]{:S(2)}) collective-permute-start(bf16[2,128,256]{2,1,0:T(8,128)(2,1)S(1)} %bitcast.244), channel_id=1, source_target_pairs={{1,0},{2,1},{3,2},{4,3},{5,4},{6,5},{7,6},{8,7},{9,8},{10,9},{11,1... | collective-permute-start | bytes 393224 | tf_op jit(solution)/shard_map/ppermute | solution.py:14
  26.3 7.1 %collective-permute-start.3 = (bf16[2,128,256]{2,1,0:T(8,128)(2,1)S(1)}, bf16[2,128,256]{2,1,0:T(8,128)(2,1)S(1)}, u32[]{:S(2)}, u32[]{:S(2)}) collective-permute-start(bf16[2,128,256]{2,1,0:T(8,128)(2,1)S(1)} %bitcast.243), channel_id=1, source_target_pairs={{2,0},{3,1},{4,2},{5,3},{6,4},{7,5},{8,6},{9,7},{10,8},{11,9},{12,... | collective-permute-start | bytes 393224 | tf_op jit(solution)/shard_map/ppermute | solution.py:14
  34.9 9.4 %copy-start.5 = (bf16[256,256]{1,0:T(8,128)(2,1)S(1)}, bf16[256,256]{1,0:T(8,128)(2,1)}, u32[]{:S(2)}) copy-start(bf16[256,256]{1,0:T(8,128)(2,1)} %param.16) | copy-start | bytes 393220
  38.3 12.4 %collective-permute-start.4 = (bf16[2,128,256]{2,1,0:T(8,128)(2,1)S(1)}, bf16[2,128,256]{2,1,0:T(8,128)(2,1)S(1)}, u32[]{:S(2)}, u32[]{:S(2)}) collective-permute-start(bf16[2,128,256]{2,1,0:T(8,128)(2,1)S(1)} %bitcast.254), channel_id=1, source_target_pairs={{0,1},{1,2},{2,3},{3,4},{4,5},{5,6},{6,7},{7,8},{8,9},{9,10},{10,1... | collective-permute-start | bytes 393224 | tf_op jit(solution)/shard_map/ppermute | solution.py:14
  41.5 9.2 %collective-permute-start.5 = (bf16[2,128,256]{2,1,0:T(8,128)(2,1)S(1)}, bf16[2,128,256]{2,1,0:T(8,128)(2,1)S(1)}, u32[]{:S(2)}, u32[]{:S(2)}) collective-permute-start(bf16[2,128,256]{2,1,0:T(8,128)(2,1)S(1)} %bitcast.253), channel_id=1, source_target_pairs={{0,2},{1,3},{2,4},{3,5},{4,6},{5,7},{6,8},{7,9},{8,10},{9,11},{10,... | collective-permute-start | bytes 393224 | tf_op jit(solution)/shard_map/ppermute | solution.py:14
  47.4 6.3 %collective-permute-start.6 = (bf16[2,128,256]{2,1,0:T(8,128)(2,1)S(1)}, bf16[2,128,256]{2,1,0:T(8,128)(2,1)S(1)}, u32[]{:S(2)}, u32[]{:S(2)}) collective-permute-start(bf16[2,128,256]{2,1,0:T(8,128)(2,1)S(1)} %bitcast.256), channel_id=1, source_target_pairs={{1,0},{2,1},{3,2},{4,3},{5,4},{6,5},{7,6},{8,7},{9,8},{10,9},{11,1... | collective-permute-start | bytes 393224 | tf_op jit(solution)/shard_map/ppermute | solution.py:14
  49.3 7.7 %collective-permute-start.7 = (bf16[2,128,256]{2,1,0:T(8,128)(2,1)S(1)}, bf16[2,128,256]{2,1,0:T(8,128)(2,1)S(1)}, u32[]{:S(2)}, u32[]{:S(2)}) collective-permute-start(bf16[2,128,256]{2,1,0:T(8,128)(2,1)S(1)} %bitcast.255), channel_id=1, source_target_pairs={{2,0},{3,1},{4,2},{5,3},{6,4},{7,5},{8,6},{9,7},{10,8},{11,9},{12,... | collective-permute-start | bytes 393224 | tf_op jit(solution)/shard_map/ppermute | solution.py:14
  57.7 1.1 copy-start.20
  67.5 13.9 %copy-start.2 = (f32[256,1,256]{0,2,1:T(8,128)S(1)}, f32[256,1,256]{0,2,1:T(8,128)}, u32[]{:S(2)}) copy-start(f32[256,1,256]{0,2,1:T(8,128)} %convolution_bitcast_fusion.2) | copy-start | bytes 786436
  67.6 14.7 %collective-permute-start.8 = (bf16[2,128,256]{2,1,0:T(8,128)(2,1)S(1)}, bf16[2,128,256]{2,1,0:T(8,128)(2,1)S(1)}, u32[]{:S(2)}, u32[]{:S(2)}) collective-permute-start(bf16[2,128,256]{2,1,0:T(8,128)(2,1)S(1)} %bitcast.249), channel_id=1, source_target_pairs={{1,0},{2,1},{3,2},{4,3},{5,4},{6,5},{7,6},{8,7},{9,8},{10,9},{11,1... | collective-permute-start | bytes 393224 | tf_op jit(solution)/shard_map/ppermute | solution.py:14
  70.3 12.2 %collective-permute-start.9 = (bf16[2,128,256]{2,1,0:T(8,128)(2,1)S(1)}, bf16[2,128,256]{2,1,0:T(8,128)(2,1)S(1)}, u32[]{:S(2)}, u32[]{:S(2)}) collective-permute-start(bf16[2,128,256]{2,1,0:T(8,128)(2,1)S(1)} %bitcast.252), channel_id=1, source_target_pairs={{2,0},{3,1},{4,2},{5,3},{6,4},{7,5},{8,6},{9,7},{10,8},{11,9},{12,... | collective-permute-start | bytes 393224 | tf_op jit(solution)/shard_map/ppermute | solution.py:14
  71.7 11.1 %collective-permute-start.10 = (bf16[2,128,256]{2,1,0:T(8,128)(2,1)S(1)}, bf16[2,128,256]{2,1,0:T(8,128)(2,1)S(1)}, u32[]{:S(2)}, u32[]{:S(2)}) collective-permute-start(bf16[2,128,256]{2,1,0:T(8,128)(2,1)S(1)} %bitcast.251), channel_id=1, source_target_pairs={{0,1},{1,2},{2,3},{3,4},{4,5},{5,6},{6,7},{7,8},{8,9},{9,10},{10,1... | collective-permute-start | bytes 393224 | tf_op jit(solution)/shard_map/ppermute | solution.py:14
  77.6 6.3 %collective-permute-start.11 = (bf16[2,128,256]{2,1,0:T(8,128)(2,1)S(1)}, bf16[2,128,256]{2,1,0:T(8,128)(2,1)S(1)}, u32[]{:S(2)}, u32[]{:S(2)}) collective-permute-start(bf16[2,128,256]{2,1,0:T(8,128)(2,1)S(1)} %bitcast.250), channel_id=1, source_target_pairs={{0,2},{1,3},{2,4},{3,5},{4,6},{5,7},{6,8},{7,9},{8,10},{9,11},{10,... | collective-permute-start | bytes 393224 | tf_op jit(solution)/shard_map/ppermute | solution.py:14
  82.3 1.8 copy-start.15
  82.3 7.0 %copy-start.13 = (s32[128]{0:T(128)S(1)}, s32[128]{0:T(128)}, u32[]{:S(2)}) copy-start(s32[128]{0:T(128)} %copy-done.12) | copy-start | bytes 1540
  84.2 21.9 %copy-start.10 = (bf16[256,256]{1,0:T(8,128)(2,1)S(1)}, bf16[256,256]{1,0:T(8,128)(2,1)}, u32[]{:S(2)}) copy-start(bf16[256,256]{1,0:T(8,128)(2,1)} %param.15) | copy-start | bytes 393220
  115.1 12.6 %copy-start.3 = (f32[256,1,256]{0,2,1:T(8,128)S(1)}, f32[256,1,256]{0,2,1:T(8,128)}, u32[]{:S(2)}) copy-start(f32[256,1,256]{0,2,1:T(8,128)} %convolution_bitcast_fusion.4) | copy-start | bytes 786436
  115.1 13.5 %collective-permute-start.12 = (bf16[2,128,256]{2,1,0:T(8,128)(2,1)S(1)}, bf16[2,128,256]{2,1,0:T(8,128)(2,1)S(1)}, u32[]{:S(2)}, u32[]{:S(2)}) collective-permute-start(bf16[2,128,256]{2,1,0:T(8,128)(2,1)S(1)} %bitcast.246), channel_id=1, source_target_pairs={{1,0},{2,1},{3,2},{4,3},{5,4},{6,5},{7,6},{8,7},{9,8},{10,9},{11,1... | collective-permute-start | bytes 393224 | tf_op jit(solution)/shard_map/ppermute | solution.py:14
  117.9 10.7 %collective-permute-start.13 = (bf16[2,128,256]{2,1,0:T(8,128)(2,1)S(1)}, bf16[2,128,256]{2,1,0:T(8,128)(2,1)S(1)}, u32[]{:S(2)}, u32[]{:S(2)}) collective-permute-start(bf16[2,128,256]{2,1,0:T(8,128)(2,1)S(1)} %bitcast.248), channel_id=1, source_target_pairs={{2,0},{3,1},{4,2},{5,3},{6,4},{7,5},{8,6},{9,7},{10,8},{11,9},{12,... | collective-permute-start | bytes 393224 | tf_op jit(solution)/shard_map/ppermute | solution.py:14
  119.2 9.9 %collective-permute-start.14 = (bf16[2,128,256]{2,1,0:T(8,128)(2,1)S(1)}, bf16[2,128,256]{2,1,0:T(8,128)(2,1)S(1)}, u32[]{:S(2)}, u32[]{:S(2)}) collective-permute-start(bf16[2,128,256]{2,1,0:T(8,128)(2,1)S(1)} %bitcast.247), channel_id=1, source_target_pairs={{0,1},{1,2},{2,3},{3,4},{4,5},{5,6},{6,7},{7,8},{8,9},{9,10},{10,1... | collective-permute-start | bytes 393224 | tf_op jit(solution)/shard_map/ppermute | solution.py:14
  123.6 6.4 %collective-permute-start.15 = (bf16[2,128,256]{2,1,0:T(8,128)(2,1)S(1)}, bf16[2,128,256]{2,1,0:T(8,128)(2,1)S(1)}, u32[]{:S(2)}, u32[]{:S(2)}) collective-permute-start(bf16[2,128,256]{2,1,0:T(8,128)(2,1)S(1)} %bitcast.245), channel_id=1, source_target_pairs={{0,2},{1,3},{2,4},{3,5},{4,6},{5,7},{6,8},{7,9},{8,10},{9,11},{10,... | collective-permute-start | bytes 393224 | tf_op jit(solution)/shard_map/ppermute | solution.py:14
  (6 other events, 4.9 us)
Sparse Core Ops, SparseCore 0:
  128.7 484.3 all-reduce.2
where the time goes:
time: 626 us; the launch traced here: 625 us
  waiting for transfers between devices  474 us (76%)
  other arithmetic  47.5 us (8%)
  starting transfers between devices  46.8 us (7%)
  local copies, waits for them, and re-layouts  27.4 us (4%)
  between operations  15.1 us (2%)
  matrix products  13.6 us (2%)
    psum x1, waiting for transfers between devices, weight_sums(): total = lax.psum(stacked, ('scen', 'graph'))  461 us
    ppermute x16, starting transfers between devices, from_behind(): lax.ppermute(value, axis, [(source, source + steps) for source in range(f...  46.7 us
    scatter-add x8, other arithmetic, backward(): accum.at[:, boundary[number], :].add(returned[number].astype(jnp.float32))  41.3 us
    ppermute x16, waiting for transfers between devices, from_behind(): lax.ppermute(value, axis, [(source, source + steps) for source in range(f...  13.2 us
  transfers between devices with their start and end apart: 17, of which 7 were waited for; matrix products, arithmetic and copies ran while one was open for 5% of the time, Pallas kernels for 0%

commit v1 on v0

v1 whole, which is shorter than its diff:
```python
import math

import jax
import jax.numpy as jnp
from jax import lax
from jax.sharding import PartitionSpec as P

shift_offsets = (1, 2, -1, -2)
REDUCE = "pp_all"


def from_behind(value, axis, steps):
    count = lax.axis_size(axis)
    first, last = (max(0, -steps), min(count, count - steps))
    return lax.ppermute(value, axis, [(source, source + steps) for source in range(first, last)])


def silu_grad(values):
    sigma = jax.nn.sigmoid(values)
    return sigma * (1.0 + values * (1.0 - sigma))


def pass_blocks(blocks, sign):
    block_rows = blocks.shape[1] // 4
    received = [
        from_behind(blocks[:, number * block_rows : (number + 1) * block_rows], "graph", sign * shift_offsets[number])
        for number in range(4)
    ]
    return jnp.concatenate(received, axis=1)


def mm(left, right, spec):
    return jnp.einsum(spec, left, right, preferred_element_type=jnp.float32)


def forward(rows, self_matrix, message_matrix, dense, select):
    sent = mm(select, rows, "mn,snd->smd").astype(jnp.bfloat16)
    extended = jnp.concatenate([rows, pass_blocks(sent, 1)], axis=1)
    message = mm(dense, extended, "nm,smd->snd").astype(jnp.bfloat16)
    pre = mm(rows, self_matrix, "snp,pw->snw") + mm(message, message_matrix, "snp,pw->snw")
    return message, pre


def backward(rows, message, pre, out_grad, self_matrix, message_matrix, dense, select):
    bus_count = rows.shape[1]
    pre_grad = (out_grad.astype(jnp.float32) * silu_grad(pre)).astype(jnp.bfloat16)
    self_sum = mm(rows, pre_grad, "snp,snw->pw")
    message_sum = mm(message, pre_grad, "snp,snw->pw")
    accum = mm(pre_grad, self_matrix, "snf,af->sna")
    message_grad = mm(pre_grad, message_matrix, "snf,af->sna").astype(jnp.bfloat16)
    tile_grad = mm(dense, message_grad, "nm,snd->smd")
    accum = accum + tile_grad[:, :bus_count]
    halo_grad = tile_grad[:, bus_count:].astype(jnp.bfloat16)
    returned = pass_blocks(halo_grad, -1)
    accum = accum + mm(select, returned, "mn,smd->snd")
    return accum.astype(jnp.bfloat16), self_sum, message_sum


def halving_scatter(data, axis):
    count = lax.axis_size(axis)
    bits = count.bit_length() - 1
    share = data.shape[0] // count
    order = [int(format(c, f"0{bits}b")[::-1], 2) for c in range(count)]
    chunks = data.reshape(count, share, *data.shape[1:])[jnp.array(order)]
    index = lax.axis_index(axis)
    for step in range(bits):
        bit = 1 << step
        half = chunks.shape[0] // 2
        mine = (index >> step) & 1
        keep = lax.dynamic_slice_in_dim(chunks, mine * half, half, 0)
        give = lax.dynamic_slice_in_dim(chunks, (1 - mine) * half, half, 0)
        got = lax.ppermute(give, axis, [(source, source ^ bit) for source in range(count)])
        chunks = keep + got
    return chunks.reshape(share, *data.shape[1:])


def doubling_sum(data, axis):
    count = lax.axis_size(axis)
    for step in range(count.bit_length() - 1):
        bit = 1 << step
        data = data + lax.ppermute(data, axis, [(source, source ^ bit) for source in range(count)])
    return data


def reduce_grads(partials, total_rows):
    width = partials.shape[0]
    graph = lax.axis_size("graph")
    scen = lax.axis_size("scen")
    share = width // graph
    scale = 1.0 / math.sqrt(total_rows)
    if REDUCE == "allreduce":
        total = lax.psum(partials, ("scen", "graph"))
        part = lax.dynamic_slice_in_dim(total, lax.axis_index("graph") * share, share, 0)
    elif REDUCE == "scatter_then_scen":
        part = lax.psum_scatter(partials, "graph", scatter_dimension=0, tiled=True)
        part = lax.psum(part, "scen")
    elif REDUCE == "scen_then_scatter":
        part = lax.psum(partials, "scen")
        part = lax.psum_scatter(part, "graph", scatter_dimension=0, tiled=True)
    elif REDUCE == "joint_scatter":
        flat = partials.reshape(graph, scen, -1)
        piece = lax.psum_scatter(flat.reshape(graph * scen, -1), ("graph", "scen"), scatter_dimension=0, tiled=True)
        part = lax.all_gather(piece, "scen", axis=0, tiled=True).reshape(share, *partials.shape[1:])
    elif REDUCE == "alltoall":
        pieces = partials.reshape(graph, share, *partials.shape[1:])
        part = lax.all_to_all(pieces, "graph", 0, 0).sum(0)
        flat = part.reshape(scen, -1)
        flat = lax.all_to_all(flat, "scen", 0, 0).sum(0)
        part = lax.all_gather(flat, "scen", axis=0, tiled=True).reshape(part.shape)
    elif REDUCE == "pp_graph_psum_scen":
        part = lax.psum(halving_scatter(partials, "graph"), "scen")
    elif REDUCE == "pp_all":
        part = doubling_sum(halving_scatter(partials, "graph"), "scen")
    else:
        raise ValueError(REDUCE)
    return part * scale


def local(
    features,
    cotangent,
    adjacency_tiles,
    tile_columns,
    boundary,
    self_weight1,
    message_weight1,
    self_weight2,
    message_weight2,
):
    adjacency = adjacency_tiles[0]
    columns = tile_columns[0]
    row_lists = boundary[0]
    tile_rows, per_row, block_rows, _ = adjacency.shape
    bus_count = features.shape[1]
    column_count = tile_rows + 4
    onehot = (columns[:, :, None] == jnp.arange(column_count, dtype=jnp.int32)).astype(jnp.bfloat16)
    dense = jnp.einsum("rjc,rjab->racb", onehot, adjacency, preferred_element_type=jnp.float32)
    dense = dense.astype(jnp.bfloat16).reshape(tile_rows * block_rows, column_count * block_rows)
    select = (row_lists.reshape(-1)[:, None] == jnp.arange(bus_count, dtype=jnp.int32)).astype(jnp.bfloat16)

    message1, pre1 = forward(features, self_weight1, message_weight1, dense, select)
    hidden = jax.nn.silu(pre1).astype(jnp.bfloat16)
    message2, pre2 = forward(hidden, self_weight2, message_weight2, dense, select)
    hidden_grad, self2, msg2 = backward(
        hidden, message2, pre2, cotangent, self_weight2, message_weight2, dense, select
    )
    input_grad, self1, msg1 = backward(
        features, message1, pre1, hidden_grad, self_weight1, message_weight1, dense, select
    )
    total_rows = features.shape[0] * bus_count * lax.axis_size("scen") * lax.axis_size("graph")
    grads = reduce_grads(jnp.stack((self1, msg1, self2, msg2), 1), total_rows)
    return (input_grad, grads[:, 0], grads[:, 1], grads[:, 2], grads[:, 3])


def solution(mesh):
    in_specs = (
        P("scen", "graph", None),
        P("scen", "graph", None),
        P("graph", None, None, None, None),
        P("graph", None, None),
        P("graph", None, None),
        P(),
        P(),
        P(),
        P(),
    )
    out_specs = (
        P("scen", "graph", None),
        P("graph", None),
        P("graph", None),
        P("graph", None),
        P("graph", None),
    )
    return jax.shard_map(local, mesh=mesh, in_specs=in_specs, out_specs=out_specs, check_vma=False)
```

time: 626 us -> 158 us (0.25)
  the two profiles are of different devices: /device:TPU:1 before, /device:TPU:12 now
where the time goes in v1:
time: 158 us; the launch traced here: 157 us
  starting transfers between devices  99.1 us (63%)
  waiting for transfers between devices  39.4 us (25%)
  matrix products  13 us (8%)
  local copies, waits for them, and re-layouts  3.53 us (2%)
    ppermute x16, starting transfers between devices, from_behind(): lax.ppermute(value, axis, [(source, source + steps) for source in range(f...  55.6 us
    ppermute x4, starting transfers between devices, doubling_sum(): lax.ppermute(data, axis, [(source, source ^ bit) for source in range(coun...  28.1 us
    ppermute x5, waiting for transfers between devices, halving_scatter(): lax.ppermute(give, axis, [(source, source ^ bit) for source in range(coun...  24.1 us
    ppermute x5, starting transfers between devices, halving_scatter(): lax.ppermute(give, axis, [(source, source ^ bit) for source in range(coun...  15.3 us
    dot_general x18, matrix products, mm(): return jnp.einsum(spec, left, right, preferred_element_type=jnp.float32)  12.6 us
    ppermute x16, waiting for transfers between devices, from_behind(): lax.ppermute(value, axis, [(source, source + steps) for source in range(f...  8.21 us
    ppermute x4, waiting for transfers between devices, doubling_sum(): lax.ppermute(data, axis, [(source, source ^ bit) for source in range(coun...  7.16 us
  transfers between devices with their start and end apart: 25, of which 12 were waited for; matrix products, arithmetic and copies ran while one was open for 3% of the time, Pallas kernels for 0%

profile of v1, /device:TPU:12, one launch (start us, length us, event | category | flops | bytes accessed | tf_op | source)
XLA Modules:
  0.0 156.8 jit_solution(10950340034276660664)
XLA Ops:
  2.8 2.0 %collective-permute-start = (bf16[2,128,256]{2,1,0:T(8,128)(2,1)}, bf16[2,128,256]{2,1,0:T(8,128)(2,1)S(1)}, u32[]{:S(2)}, u32[]{:S(2)}) collective-permute-start(bf16[2,128,256]{2,1,0:T(8,128)(2,1)} %get-tuple-element.22), channel_id=1, source_target_pairs={{0,1},{1,2},{2,3},{3,4},{4,5},{5,6},{6,7},{7,8},{8,9},{9,10},{10,1... | collective-permute-start | bytes 393224 | tf_op jit(solution)/shard_map/ppermute | solution.py:15
  4.8 3.8 %collective-permute-start.1 = (bf16[2,128,256]{2,1,0:T(8,128)(2,1)}, bf16[2,128,256]{2,1,0:T(8,128)(2,1)S(1)}, u32[]{:S(2)}, u32[]{:S(2)}) collective-permute-start(bf16[2,128,256]{2,1,0:T(8,128)(2,1)} %get-tuple-element.21), channel_id=1, source_target_pairs={{0,2},{1,3},{2,4},{3,5},{4,6},{5,7},{6,8},{7,9},{8,10},{9,11},{10,... | collective-permute-start | bytes 393224 | tf_op jit(solution)/shard_map/ppermute | solution.py:15
  8.7 6.1 %collective-permute-start.2 = (bf16[2,128,256]{2,1,0:T(8,128)(2,1)S(1)}, bf16[2,128,256]{2,1,0:T(8,128)(2,1)S(1)}, u32[]{:S(2)}, u32[]{:S(2)}) collective-permute-start(bf16[2,128,256]{2,1,0:T(8,128)(2,1)S(1)} %get-tuple-element.20), channel_id=1, source_target_pairs={{1,0},{2,1},{3,2},{4,3},{5,4},{6,5},{7,6},{8,7},{9,8},{10,9},{11,1... | collective-permute-start | bytes 393224 | tf_op jit(solution)/shard_map/ppermute | solution.py:15
  14.7 2.1 %collective-permute-start.3 = (bf16[2,128,256]{2,1,0:T(8,128)(2,1)S(1)}, bf16[2,128,256]{2,1,0:T(8,128)(2,1)S(1)}, u32[]{:S(2)}, u32[]{:S(2)}) collective-permute-start(bf16[2,128,256]{2,1,0:T(8,128)(2,1)S(1)} %get-tuple-element.19), channel_id=1, source_target_pairs={{2,0},{3,1},{4,2},{5,3},{6,4},{7,5},{8,6},{9,7},{10,8},{11,9},{12,... | collective-permute-start | bytes 393224 | tf_op jit(solution)/shard_map/ppermute | solution.py:15
  18.8 2.8 %collective-permute-done.3 = bf16[2,128,256]{2,1,0:T(8,128)(2,1)S(1)} collective-permute-done((bf16[2,128,256]{2,1,0:T(8,128)(2,1)S(1)}, bf16[2,128,256]{2,1,0:T(8,128)(2,1)S(1)}, u32[]{:S(2)}, u32[]{:S(2)}) %collective-permute-start.3) | collective-permute-done | bytes 131104 | tf_op jit(solution)/shard_map/ppermute | solution.py:15
  25.6 2.1 %collective-permute-start.5 = (bf16[2,128,256]{2,1,0:T(8,128)(2,1)S(1)}, bf16[2,128,256]{2,1,0:T(8,128)(2,1)S(1)}, u32[]{:S(2)}, u32[]{:S(2)}) collective-permute-start(bf16[2,128,256]{2,1,0:T(8,128)(2,1)S(1)} %get-tuple-element.17), channel_id=1, source_target_pairs={{0,2},{1,3},{2,4},{3,5},{4,6},{5,7},{6,8},{7,9},{8,10},{9,11},{10,... | collective-permute-start | bytes 393224 | tf_op jit(solution)/shard_map/ppermute | solution.py:15
  27.9 6.3 %collective-permute-start.6 = (bf16[2,128,256]{2,1,0:T(8,128)(2,1)S(1)}, bf16[2,128,256]{2,1,0:T(8,128)(2,1)S(1)}, u32[]{:S(2)}, u32[]{:S(2)}) collective-permute-start(bf16[2,128,256]{2,1,0:T(8,128)(2,1)S(1)} %get-tuple-element.16), channel_id=1, source_target_pairs={{1,0},{2,1},{3,2},{4,3},{5,4},{6,5},{7,6},{8,7},{9,8},{10,9},{11,1... | collective-permute-start | bytes 393224 | tf_op jit(solution)/shard_map/ppermute | solution.py:15
  34.3 3.6 %collective-permute-start.7 = (bf16[2,128,256]{2,1,0:T(8,128)(2,1)S(1)}, bf16[2,128,256]{2,1,0:T(8,128)(2,1)S(1)}, u32[]{:S(2)}, u32[]{:S(2)}) collective-permute-start(bf16[2,128,256]{2,1,0:T(8,128)(2,1)S(1)} %get-tuple-element.15), channel_id=1, source_target_pairs={{2,0},{3,1},{4,2},{5,3},{6,4},{7,5},{8,6},{9,7},{10,8},{11,9},{12,... | collective-permute-start | bytes 393224 | tf_op jit(solution)/shard_map/ppermute | solution.py:15
  38.0 3.1 %collective-permute-done.7 = bf16[2,128,256]{2,1,0:T(8,128)(2,1)S(1)} collective-permute-done((bf16[2,128,256]{2,1,0:T(8,128)(2,1)S(1)}, bf16[2,128,256]{2,1,0:T(8,128)(2,1)S(1)}, u32[]{:S(2)}, u32[]{:S(2)}) %collective-permute-start.7) | collective-permute-done | bytes 131104 | tf_op jit(solution)/shard_map/ppermute | solution.py:15
  42.0 2.4 %fusion.57 = (bf16[2,768,256]{2,1,0:T(8,128)(2,1)}, f32[2,768,256]{2,1,0:T(8,128)S(1)}) fusion(bf16[256,768,1]{1,0,2:T(8,128)(2,1)S(1)} %reshape.40, bf16[2,256,256]{2,1,0:T(8,128)(2,1)S(1)} %multiply_convert_fusion, bf16[256,256]{1,0:T(8,128)(2,1)} %param.18), kind=kOutput, calls=%fused_computation.102 | convolution fusion | flops 268959744 | bytes 3145728 | tf_op jit(solution)/shard_map/nm,snd->smd/dot_general | solution.py:33
  46.0 2.6 %collective-permute-start.11 = (bf16[2,128,256]{2,1,0:T(8,128)(2,1)S(1)}, bf16[2,128,256]{2,1,0:T(8,128)(2,1)S(1)}, u32[]{:S(2)}, u32[]{:S(2)}) collective-permute-start(bf16[2,128,256]{2,1,0:T(8,128)(2,1)S(1)} %get-tuple-element.12), channel_id=1, source_target_pairs={{0,2},{1,3},{2,4},{3,5},{4,6},{5,7},{6,8},{7,9},{8,10},{9,11},{10,... | collective-permute-start | bytes 393224 | tf_op jit(solution)/shard_map/ppermute | solution.py:15
  50.6 5.9 %collective-permute-start.9 = (bf16[2,128,256]{2,1,0:T(8,128)(2,1)S(1)}, bf16[2,128,256]{2,1,0:T(8,128)(2,1)S(1)}, u32[]{:S(2)}, u32[]{:S(2)}) collective-permute-start(bf16[2,128,256]{2,1,0:T(8,128)(2,1)S(1)} %get-tuple-element.14), channel_id=1, source_target_pairs={{2,0},{3,1},{4,2},{5,3},{6,4},{7,5},{8,6},{9,7},{10,8},{11,9},{12,... | collective-permute-start | bytes 393224 | tf_op jit(solution)/shard_map/ppermute | solution.py:15
  56.5 3.4 %collective-permute-start.8 = (bf16[2,128,256]{2,1,0:T(8,128)(2,1)S(1)}, bf16[2,128,256]{2,1,0:T(8,128)(2,1)S(1)}, u32[]{:S(2)}, u32[]{:S(2)}) collective-permute-start(bf16[2,128,256]{2,1,0:T(8,128)(2,1)S(1)} %get-tuple-element.11), channel_id=1, source_target_pairs={{1,0},{2,1},{3,2},{4,3},{5,4},{6,5},{7,6},{8,7},{9,8},{10,9},{11,1... | collective-permute-start | bytes 393224 | tf_op jit(solution)/shard_map/ppermute | solution.py:15
  60.2 2.2 %collective-permute-done.8 = bf16[2,128,256]{2,1,0:T(8,128)(2,1)S(1)} collective-permute-done((bf16[2,128,256]{2,1,0:T(8,128)(2,1)S(1)}, bf16[2,128,256]{2,1,0:T(8,128)(2,1)S(1)}, u32[]{:S(2)}, u32[]{:S(2)}) %collective-permute-start.8) | collective-permute-done | bytes 131104 | tf_op jit(solution)/shard_map/ppermute | solution.py:15
  64.2 2.9 %collective-permute-start.16 = (f32[16,8,4,256]{3,1,2,0:T(8,128)S(1)}, f32[16,8,4,256]{3,1,2,0:T(8,128)S(1)}, u32[]{:S(2)}, u32[]{:S(2)}) collective-permute-start(f32[16,8,4,256]{3,1,2,0:T(8,128)S(1)} %constant_dynamic-slice_fusion.3), channel_id=1, source_target_pairs={{0,1},{1,0},{2,3},{3,2},{4,5},{5,4},{6,7},{7,6},{8,9},{9,8},{10,11... | collective-permute-start | bytes 1572872 | tf_op jit(solution)/shard_map/ppermute | solution.py:72
  68.7 2.4 %collective-permute-start.17 = (f32[8,8,4,256]{3,1,2,0:T(8,128)S(1)}, f32[8,8,4,256]{3,1,2,0:T(8,128)S(1)}, u32[]{:S(2)}, u32[]{:S(2)}) collective-permute-start(f32[8,8,4,256]{3,1,2,0:T(8,128)S(1)} %constant_dynamic-slice_fusion.2), channel_id=1, source_target_pairs={{0,2},{1,3},{2,0},{3,1},{4,6},{5,7},{6,4},{7,5},{8,10},{9,11},{10,... | collective-permute-start | bytes 786440 | tf_op jit(solution)/shard_map/ppermute | solution.py:72
  71.1 8.0 %collective-permute-done.17 = f32[8,8,4,256]{3,1,2,0:T(8,128)S(1)} collective-permute-done((f32[8,8,4,256]{3,1,2,0:T(8,128)S(1)}, f32[8,8,4,256]{3,1,2,0:T(8,128)S(1)}, u32[]{:S(2)}, u32[]{:S(2)}) %collective-permute-start.17) | collective-permute-done | bytes 262176 | tf_op jit(solution)/shard_map/ppermute | solution.py:72
  79.2 4.9 %collective-permute-start.18 = (f32[4,8,4,256]{3,1,2,0:T(8,128)S(1)}, f32[4,8,4,256]{3,1,2,0:T(8,128)S(1)}, u32[]{:S(2)}, u32[]{:S(2)}) collective-permute-start(f32[4,8,4,256]{3,1,2,0:T(8,128)S(1)} %constant_dynamic-slice_fusion.1), channel_id=1, source_target_pairs={{0,4},{1,5},{2,6},{3,7},{4,0},{5,1},{6,2},{7,3},{8,12},{9,13},{10,... | collective-permute-start | bytes 393224 | tf_op jit(solution)/shard_map/ppermute | solution.py:72
  84.1 6.2 %collective-permute-done.18 = f32[4,8,4,256]{3,1,2,0:T(8,128)S(1)} collective-permute-done((f32[4,8,4,256]{3,1,2,0:T(8,128)S(1)}, f32[4,8,4,256]{3,1,2,0:T(8,128)S(1)}, u32[]{:S(2)}, u32[]{:S(2)}) %collective-permute-start.18) | collective-permute-done | bytes 131104 | tf_op jit(solution)/shard_map/ppermute | solution.py:72
  90.4 2.4 %collective-permute-start.19 = (f32[2,8,4,256]{3,1,2,0:T(8,128)S(1)}, f32[2,8,4,256]{3,1,2,0:T(8,128)S(1)}, u32[]{:S(2)}, u32[]{:S(2)}) collective-permute-start(f32[2,8,4,256]{3,1,2,0:T(8,128)S(1)} %constant_dynamic-slice_fusion), channel_id=1, source_target_pairs={{0,8},{1,9},{2,10},{3,11},{4,12},{5,13},{6,14},{7,15},{8,0},{9,1},... | collective-permute-start | bytes 196616 | tf_op jit(solution)/shard_map/ppermute | solution.py:72
  92.8 3.8 %collective-permute-done.19 = f32[2,8,4,256]{3,1,2,0:T(8,128)S(1)} collective-permute-done((f32[2,8,4,256]{3,1,2,0:T(8,128)S(1)}, f32[2,8,4,256]{3,1,2,0:T(8,128)S(1)}, u32[]{:S(2)}, u32[]{:S(2)}) %collective-permute-start.19) | collective-permute-done | bytes 65568 | tf_op jit(solution)/shard_map/ppermute | solution.py:72
  96.6 2.8 %collective-permute-start.20 = (f32[1,8,4,256]{3,1,2,0:T(8,128)S(1)}, f32[1,8,4,256]{3,1,2,0:T(8,128)S(1)}, u32[]{:S(2)}, u32[]{:S(2)}) collective-permute-start(f32[1,8,4,256]{3,1,2,0:T(8,128)S(1)} %constant_dynamic-slice_fusion.4), channel_id=1, source_target_pairs={{0,16},{1,17},{2,18},{3,19},{4,20},{5,21},{6,22},{7,23},{8,24},{9,... | collective-permute-start | bytes 98312 | tf_op jit(solution)/shard_map/ppermute | solution.py:72
  99.4 4.5 %collective-permute-done.20 = f32[1,8,4,256]{3,1,2,0:T(8,128)S(1)} collective-permute-done((f32[1,8,4,256]{3,1,2,0:T(8,128)S(1)}, f32[1,8,4,256]{3,1,2,0:T(8,128)S(1)}, u32[]{:S(2)}, u32[]{:S(2)}) %collective-permute-start.20) | collective-permute-done | bytes 32800 | tf_op jit(solution)/shard_map/ppermute | solution.py:72
  103.9 9.2 %collective-permute-start.21 = (f32[8,4,256]{2,0,1:T(8,128)S(1)}, f32[8,4,256]{2,0,1:T(8,128)S(1)}, u32[]{:S(2)}, u32[]{:S(2)}) collective-permute-start(f32[8,4,256]{2,0,1:T(8,128)S(1)} %add_bitcast_fusion), channel_id=1, source_target_pairs={{0,32},{32,0},{64,96},{96,64},{128,160},{160,128},{192,224},{224,1... | collective-permute-start | bytes 98312 | tf_op jit(solution)/shard_map/ppermute | solution.py:81
  115.7 13.4 %collective-permute-start.22 = (f32[8,4,256]{2,0,1:T(8,128)S(1)}, f32[8,4,256]{2,0,1:T(8,128)S(1)}, u32[]{:S(2)}, u32[]{:S(2)}) collective-permute-start(f32[8,4,256]{2,0,1:T(8,128)S(1)} %add.123), channel_id=1, source_target_pairs={{0,64},{32,96},{64,0},{96,32},{128,192},{160,224},{192,128},{224,1... | collective-permute-start | bytes 98312 | tf_op jit(solution)/shard_map/ppermute | solution.py:81
  129.1 2.1 %collective-permute-start.15 = (bf16[2,128,256]{2,1,0:T(8,128)(2,1)S(1)}, bf16[2,128,256]{2,1,0:T(8,128)(2,1)S(1)}, u32[]{:S(2)}, u32[]{:S(2)}) collective-permute-start(bf16[2,128,256]{2,1,0:T(8,128)(2,1)S(1)} %get-tuple-element.8), channel_id=1, source_target_pairs={{0,2},{1,3},{2,4},{3,5},{4,6},{5,7},{6,8},{7,9},{8,10},{9,11},{10,... | collective-permute-start | bytes 393224 | tf_op jit(solution)/shard_map/ppermute | solution.py:15
  133.2 6.4 %collective-permute-start.13 = (bf16[2,128,256]{2,1,0:T(8,128)(2,1)S(1)}, bf16[2,128,256]{2,1,0:T(8,128)(2,1)S(1)}, u32[]{:S(2)}, u32[]{:S(2)}) collective-permute-start(bf16[2,128,256]{2,1,0:T(8,128)(2,1)S(1)} %get-tuple-element.10), channel_id=1, source_target_pairs={{2,0},{3,1},{4,2},{5,3},{6,4},{7,5},{8,6},{9,7},{10,8},{11,9},{12,... | collective-permute-start | bytes 393224 | tf_op jit(solution)/shard_map/ppermute | solution.py:15
  139.6 3.4 %collective-permute-start.12 = (bf16[2,128,256]{2,1,0:T(8,128)(2,1)S(1)}, bf16[2,128,256]{2,1,0:T(8,128)(2,1)S(1)}, u32[]{:S(2)}, u32[]{:S(2)}) collective-permute-start(bf16[2,128,256]{2,1,0:T(8,128)(2,1)S(1)} %get-tuple-element.7), channel_id=1, source_target_pairs={{1,0},{2,1},{3,2},{4,3},{5,4},{6,5},{7,6},{8,7},{9,8},{10,9},{11,1... | collective-permute-start | bytes 393224 | tf_op jit(solution)/shard_map/ppermute | solution.py:15
  143.0 3.1 %collective-permute-start.23 = (f32[8,4,256]{2,0,1:T(8,128)S(1)}, f32[8,4,256]{2,0,1:T(8,128)S(1)}, u32[]{:S(2)}, u32[]{:S(2)}) collective-permute-start(f32[8,4,256]{2,0,1:T(8,128)S(1)} %add.124), channel_id=1, source_target_pairs={{0,128},{32,160},{64,192},{96,224},{128,0},{160,32},{192,64},{224,... | collective-permute-start | bytes 98312 | tf_op jit(solution)/shard_map/ppermute | solution.py:81
  146.4 2.4 %collective-permute-done.23 = f32[8,4,256]{2,0,1:T(8,128)S(1)} collective-permute-done((f32[8,4,256]{2,0,1:T(8,128)S(1)}, f32[8,4,256]{2,0,1:T(8,128)S(1)}, u32[]{:S(2)}, u32[]{:S(2)}) %collective-permute-start.23) | collective-permute-done | bytes 32800 | tf_op jit(solution)/shard_map/ppermute | solution.py:81
  148.8 2.4 %collective-permute-start.24 = (f32[8,4,256]{2,0,1:T(8,128)S(1)}, f32[8,4,256]{2,0,1:T(8,128)S(1)}, u32[]{:S(2)}, u32[]{:S(2)}) collective-permute-start(f32[8,4,256]{2,0,1:T(8,128)S(1)} %add.125), channel_id=1, source_target_pairs={{0,256},{32,288},{64,320},{96,352},{128,384},{160,416},{192,448},{... | collective-permute-start | bytes 98312 | tf_op jit(solution)/shard_map/ppermute | solution.py:81
  152.4 3.7 %collective-permute-done.24 = f32[8,4,256]{2,0,1:T(8,128)S(1)} collective-permute-done((f32[8,4,256]{2,0,1:T(8,128)S(1)}, f32[8,4,256]{2,0,1:T(8,128)S(1)}, u32[]{:S(2)}, u32[]{:S(2)}) %collective-permute-start.24) | collective-permute-done | bytes 32800 | tf_op jit(solution)/shard_map/ppermute | solution.py:81
  (100 shorter events, 22.8 us)
Async XLA Ops:
  0.6 16.6 %copy-start = (bf16[1,2,4,128,128]{4,3,2,1,0:T(8,128)(2,1)S(1)}, bf16[1,2,4,128,128]{4,3,2,1,0:T(8,128)(2,1)}, u32[]{:S(2)}) copy-start(bf16[1,2,4,128,128]{4,3,2,1,0:T(8,128)(2,1)} %param.12) | copy-start | bytes 786436
  0.6 16.2 %copy-start.1 = (bf16[2,256,256]{2,1,0:T(8,128)(2,1)S(1)}, bf16[2,256,256]{2,1,0:T(8,128)(2,1)}, u32[]{:S(2)}) copy-start(bf16[2,256,256]{2,1,0:T(8,128)(2,1)} %param.10) | copy-start | bytes 786436
  0.7 16.3 %copy-start.4 = (bf16[256,256]{1,0:T(8,128)(2,1)S(1)}, bf16[256,256]{1,0:T(8,128)(2,1)}, u32[]{:S(2)}) copy-start(bf16[256,256]{1,0:T(8,128)(2,1)} %param.15) | copy-start | bytes 393220
  0.7 16.6 %copy-start.9 = (s32[1,2,4]{2,1,0:T(2,128)S(1)}, s32[1,2,4]{2,1,0:T(2,128)}, u32[]{:S(2)}) copy-start(s32[1,2,4]{2,1,0:T(2,128)} %param.13) | copy-start | bytes 100
  2.8 15.5 %collective-permute-start = (bf16[2,128,256]{2,1,0:T(8,128)(2,1)}, bf16[2,128,256]{2,1,0:T(8,128)(2,1)S(1)}, u32[]{:S(2)}, u32[]{:S(2)}) collective-permute-start(bf16[2,128,256]{2,1,0:T(8,128)(2,1)} %get-tuple-element.22), channel_id=1, source_target_pairs={{0,1},{1,2},{2,3},{3,4},{4,5},{5,6},{6,7},{7,8},{8,9},{9,10},{10,1... | collective-permute-start | bytes 393224 | tf_op jit(solution)/shard_map/ppermute | solution.py:15
  4.8 13.6 %collective-permute-start.1 = (bf16[2,128,256]{2,1,0:T(8,128)(2,1)}, bf16[2,128,256]{2,1,0:T(8,128)(2,1)S(1)}, u32[]{:S(2)}, u32[]{:S(2)}) collective-permute-start(bf16[2,128,256]{2,1,0:T(8,128)(2,1)} %get-tuple-element.21), channel_id=1, source_target_pairs={{0,2},{1,3},{2,4},{3,5},{4,6},{5,7},{6,8},{7,9},{8,10},{9,11},{10,... | collective-permute-start | bytes 393224 | tf_op jit(solution)/shard_map/ppermute | solution.py:15
  8.7 9.9 %collective-permute-start.2 = (bf16[2,128,256]{2,1,0:T(8,128)(2,1)S(1)}, bf16[2,128,256]{2,1,0:T(8,128)(2,1)S(1)}, u32[]{:S(2)}, u32[]{:S(2)}) collective-permute-start(bf16[2,128,256]{2,1,0:T(8,128)(2,1)S(1)} %get-tuple-element.20), channel_id=1, source_target_pairs={{1,0},{2,1},{3,2},{4,3},{5,4},{6,5},{7,6},{8,7},{9,8},{10,9},{11,1... | collective-permute-start | bytes 393224 | tf_op jit(solution)/shard_map/ppermute | solution.py:15
  14.7 6.9 %collective-permute-start.3 = (bf16[2,128,256]{2,1,0:T(8,128)(2,1)S(1)}, bf16[2,128,256]{2,1,0:T(8,128)(2,1)S(1)}, u32[]{:S(2)}, u32[]{:S(2)}) collective-permute-start(bf16[2,128,256]{2,1,0:T(8,128)(2,1)S(1)} %get-tuple-element.19), channel_id=1, source_target_pairs={{2,0},{3,1},{4,2},{5,3},{6,4},{7,5},{8,6},{9,7},{10,8},{11,9},{12,... | collective-permute-start | bytes 393224 | tf_op jit(solution)/shard_map/ppermute | solution.py:15
  23.7 14.2 %collective-permute-start.4 = (bf16[2,128,256]{2,1,0:T(8,128)(2,1)S(1)}, bf16[2,128,256]{2,1,0:T(8,128)(2,1)S(1)}, u32[]{:S(2)}, u32[]{:S(2)}) collective-permute-start(bf16[2,128,256]{2,1,0:T(8,128)(2,1)S(1)} %get-tuple-element.18), channel_id=1, source_target_pairs={{0,1},{1,2},{2,3},{3,4},{4,5},{5,6},{6,7},{7,8},{8,9},{9,10},{10,1... | collective-permute-start | bytes 393224 | tf_op jit(solution)/shard_map/ppermute | solution.py:15
  25.6 16.0 %copy-start.6 = (bf16[256,256]{1,0:T(8,128)(2,1)S(1)}, bf16[256,256]{1,0:T(8,128)(2,1)}, u32[]{:S(2)}) copy-start(bf16[256,256]{1,0:T(8,128)(2,1)} %param.18) | copy-start | bytes 393220
  25.6 12.3 %collective-permute-start.5 = (bf16[2,128,256]{2,1,0:T(8,128)(2,1)S(1)}, bf16[2,128,256]{2,1,0:T(8,128)(2,1)S(1)}, u32[]{:S(2)}, u32[]{:S(2)}) collective-permute-start(bf16[2,128,256]{2,1,0:T(8,128)(2,1)S(1)} %get-tuple-element.17), channel_id=1, source_target_pairs={{0,2},{1,3},{2,4},{3,5},{4,6},{5,7},{6,8},{7,9},{8,10},{9,11},{10,... | collective-permute-start | bytes 393224 | tf_op jit(solution)/shard_map/ppermute | solution.py:15
  27.9 10.1 %collective-permute-start.6 = (bf16[2,128,256]{2,1,0:T(8,128)(2,1)S(1)}, bf16[2,128,256]{2,1,0:T(8,128)(2,1)S(1)}, u32[]{:S(2)}, u32[]{:S(2)}) collective-permute-start(bf16[2,128,256]{2,1,0:T(8,128)(2,1)S(1)} %get-tuple-element.16), channel_id=1, source_target_pairs={{1,0},{2,1},{3,2},{4,3},{5,4},{6,5},{7,6},{8,7},{9,8},{10,9},{11,1... | collective-permute-start | bytes 393224 | tf_op jit(solution)/shard_map/ppermute | solution.py:15
  34.3 6.9 %collective-permute-start.7 = (bf16[2,128,256]{2,1,0:T(8,128)(2,1)S(1)}, bf16[2,128,256]{2,1,0:T(8,128)(2,1)S(1)}, u32[]{:S(2)}, u32[]{:S(2)}) collective-permute-start(bf16[2,128,256]{2,1,0:T(8,128)(2,1)S(1)} %get-tuple-element.15), channel_id=1, source_target_pairs={{2,0},{3,1},{4,2},{5,3},{6,4},{7,5},{8,6},{9,7},{10,8},{11,9},{12,... | collective-permute-start | bytes 393224 | tf_op jit(solution)/shard_map/ppermute | solution.py:15
  44.7 17.6 %copy-start.12 = (f32[2,256,256]{2,1,0:T(8,128)S(1)}, f32[2,256,256]{2,1,0:T(8,128)}, u32[]{:S(2)}) copy-start(f32[2,256,256]{2,1,0:T(8,128)} %get-tuple-element.27) | copy-start | bytes 1572868
  46.0 14.1 %collective-permute-start.11 = (bf16[2,128,256]{2,1,0:T(8,128)(2,1)S(1)}, bf16[2,128,256]{2,1,0:T(8,128)(2,1)S(1)}, u32[]{:S(2)}, u32[]{:S(2)}) collective-permute-start(bf16[2,128,256]{2,1,0:T(8,128)(2,1)S(1)} %get-tuple-element.12), channel_id=1, source_target_pairs={{0,2},{1,3},{2,4},{3,5},{4,6},{5,7},{6,8},{7,9},{8,10},{9,11},{10,... | collective-permute-start | bytes 393224 | tf_op jit(solution)/shard_map/ppermute | solution.py:15
  48.6 11.5 %collective-permute-start.10 = (bf16[2,128,256]{2,1,0:T(8,128)(2,1)S(1)}, bf16[2,128,256]{2,1,0:T(8,128)(2,1)S(1)}, u32[]{:S(2)}, u32[]{:S(2)}) collective-permute-start(bf16[2,128,256]{2,1,0:T(8,128)(2,1)S(1)} %get-tuple-element.13), channel_id=1, source_target_pairs={{0,1},{1,2},{2,3},{3,4},{4,5},{5,6},{6,7},{7,8},{8,9},{9,10},{10,1... | collective-permute-start | bytes 393224 | tf_op jit(solution)/shard_map/ppermute | solution.py:15
  50.6 9.6 %collective-permute-start.9 = (bf16[2,128,256]{2,1,0:T(8,128)(2,1)S(1)}, bf16[2,128,256]{2,1,0:T(8,128)(2,1)S(1)}, u32[]{:S(2)}, u32[]{:S(2)}) collective-permute-start(bf16[2,128,256]{2,1,0:T(8,128)(2,1)S(1)} %get-tuple-element.14), channel_id=1, source_target_pairs={{2,0},{3,1},{4,2},{5,3},{6,4},{7,5},{8,6},{9,7},{10,8},{11,9},{12,... | collective-permute-start | bytes 393224 | tf_op jit(solution)/shard_map/ppermute | solution.py:15
  56.5 5.9 %collective-permute-start.8 = (bf16[2,128,256]{2,1,0:T(8,128)(2,1)S(1)}, bf16[2,128,256]{2,1,0:T(8,128)(2,1)S(1)}, u32[]{:S(2)}, u32[]{:S(2)}) collective-permute-start(bf16[2,128,256]{2,1,0:T(8,128)(2,1)S(1)} %get-tuple-element.11), channel_id=1, source_target_pairs={{1,0},{2,1},{3,2},{4,3},{5,4},{6,5},{7,6},{8,7},{9,8},{10,9},{11,1... | collective-permute-start | bytes 393224 | tf_op jit(solution)/shard_map/ppermute | solution.py:15
  64.2 4.4 %collective-permute-start.16 = (f32[16,8,4,256]{3,1,2,0:T(8,128)S(1)}, f32[16,8,4,256]{3,1,2,0:T(8,128)S(1)}, u32[]{:S(2)}, u32[]{:S(2)}) collective-permute-start(f32[16,8,4,256]{3,1,2,0:T(8,128)S(1)} %constant_dynamic-slice_fusion.3), channel_id=1, source_target_pairs={{0,1},{1,0},{2,3},{3,2},{4,5},{5,4},{6,7},{7,6},{8,9},{9,8},{10,11... | collective-permute-start | bytes 1572872 | tf_op jit(solution)/shard_map/ppermute | solution.py:72
  68.7 10.5 %collective-permute-start.17 = (f32[8,8,4,256]{3,1,2,0:T(8,128)S(1)}, f32[8,8,4,256]{3,1,2,0:T(8,128)S(1)}, u32[]{:S(2)}, u32[]{:S(2)}) collective-permute-start(f32[8,8,4,256]{3,1,2,0:T(8,128)S(1)} %constant_dynamic-slice_fusion.2), channel_id=1, source_target_pairs={{0,2},{1,3},{2,0},{3,1},{4,6},{5,7},{6,4},{7,5},{8,10},{9,11},{10,... | collective-permute-start | bytes 786440 | tf_op jit(solution)/shard_map/ppermute | solution.py:72
  79.2 11.1 %collective-permute-start.18 = (f32[4,8,4,256]{3,1,2,0:T(8,128)S(1)}, f32[4,8,4,256]{3,1,2,0:T(8,128)S(1)}, u32[]{:S(2)}, u32[]{:S(2)}) collective-permute-start(f32[4,8,4,256]{3,1,2,0:T(8,128)S(1)} %constant_dynamic-slice_fusion.1), channel_id=1, source_target_pairs={{0,4},{1,5},{2,6},{3,7},{4,0},{5,1},{6,2},{7,3},{8,12},{9,13},{10,... | collective-permute-start | bytes 393224 | tf_op jit(solution)/shard_map/ppermute | solution.py:72
  90.4 6.2 %collective-permute-start.19 = (f32[2,8,4,256]{3,1,2,0:T(8,128)S(1)}, f32[2,8,4,256]{3,1,2,0:T(8,128)S(1)}, u32[]{:S(2)}, u32[]{:S(2)}) collective-permute-start(f32[2,8,4,256]{3,1,2,0:T(8,128)S(1)} %constant_dynamic-slice_fusion), channel_id=1, source_target_pairs={{0,8},{1,9},{2,10},{3,11},{4,12},{5,13},{6,14},{7,15},{8,0},{9,1},... | collective-permute-start | bytes 196616 | tf_op jit(solution)/shard_map/ppermute | solution.py:72
  96.6 7.3 %collective-permute-start.20 = (f32[1,8,4,256]{3,1,2,0:T(8,128)S(1)}, f32[1,8,4,256]{3,1,2,0:T(8,128)S(1)}, u32[]{:S(2)}, u32[]{:S(2)}) collective-permute-start(f32[1,8,4,256]{3,1,2,0:T(8,128)S(1)} %constant_dynamic-slice_fusion.4), channel_id=1, source_target_pairs={{0,16},{1,17},{2,18},{3,19},{4,20},{5,21},{6,22},{7,23},{8,24},{9,... | collective-permute-start | bytes 98312 | tf_op jit(solution)/shard_map/ppermute | solution.py:72
  103.9 42.2 %copy-start.5 = (bf16[256,256]{1,0:T(8,128)(2,1)S(1)}, bf16[256,256]{1,0:T(8,128)(2,1)}, u32[]{:S(2)}) copy-start(bf16[256,256]{1,0:T(8,128)(2,1)} %param.15) | copy-start | bytes 393220
  103.9 11.8 %collective-permute-start.21 = (f32[8,4,256]{2,0,1:T(8,128)S(1)}, f32[8,4,256]{2,0,1:T(8,128)S(1)}, u32[]{:S(2)}, u32[]{:S(2)}) collective-permute-start(f32[8,4,256]{2,0,1:T(8,128)S(1)} %add_bitcast_fusion), channel_id=1, source_target_pairs={{0,32},{32,0},{64,96},{96,64},{128,160},{160,128},{192,224},{224,1... | collective-permute-start | bytes 98312 | tf_op jit(solution)/shard_map/ppermute | solution.py:81
  115.7 27.3 %collective-permute-start.22 = (f32[8,4,256]{2,0,1:T(8,128)S(1)}, f32[8,4,256]{2,0,1:T(8,128)S(1)}, u32[]{:S(2)}, u32[]{:S(2)}) collective-permute-start(f32[8,4,256]{2,0,1:T(8,128)S(1)} %add.123), channel_id=1, source_target_pairs={{0,64},{32,96},{64,0},{96,32},{128,192},{160,224},{192,128},{224,1... | collective-permute-start | bytes 98312 | tf_op jit(solution)/shard_map/ppermute | solution.py:81
  129.1 22.1 %collective-permute-start.15 = (bf16[2,128,256]{2,1,0:T(8,128)(2,1)S(1)}, bf16[2,128,256]{2,1,0:T(8,128)(2,1)S(1)}, u32[]{:S(2)}, u32[]{:S(2)}) collective-permute-start(bf16[2,128,256]{2,1,0:T(8,128)(2,1)S(1)} %get-tuple-element.8), channel_id=1, source_target_pairs={{0,2},{1,3},{2,4},{3,5},{4,6},{5,7},{6,8},{7,9},{8,10},{9,11},{10,... | collective-permute-start | bytes 393224 | tf_op jit(solution)/shard_map/ppermute | solution.py:15
  131.3 20.0 %collective-permute-start.14 = (bf16[2,128,256]{2,1,0:T(8,128)(2,1)S(1)}, bf16[2,128,256]{2,1,0:T(8,128)(2,1)S(1)}, u32[]{:S(2)}, u32[]{:S(2)}) collective-permute-start(bf16[2,128,256]{2,1,0:T(8,128)(2,1)S(1)} %get-tuple-element.9), channel_id=1, source_target_pairs={{0,1},{1,2},{2,3},{3,4},{4,5},{5,6},{6,7},{7,8},{8,9},{9,10},{10,1... | collective-permute-start | bytes 393224 | tf_op jit(solution)/shard_map/ppermute | solution.py:15
  133.2 18.1 %collective-permute-start.13 = (bf16[2,128,256]{2,1,0:T(8,128)(2,1)S(1)}, bf16[2,128,256]{2,1,0:T(8,128)(2,1)S(1)}, u32[]{:S(2)}, u32[]{:S(2)}) collective-permute-start(bf16[2,128,256]{2,1,0:T(8,128)(2,1)S(1)} %get-tuple-element.10), channel_id=1, source_target_pairs={{2,0},{3,1},{4,2},{5,3},{6,4},{7,5},{8,6},{9,7},{10,8},{11,9},{12,... | collective-permute-start | bytes 393224 | tf_op jit(solution)/shard_map/ppermute | solution.py:15
  139.6 11.7 %collective-permute-start.12 = (bf16[2,128,256]{2,1,0:T(8,128)(2,1)S(1)}, bf16[2,128,256]{2,1,0:T(8,128)(2,1)S(1)}, u32[]{:S(2)}, u32[]{:S(2)}) collective-permute-start(bf16[2,128,256]{2,1,0:T(8,128)(2,1)S(1)} %get-tuple-element.7), channel_id=1, source_target_pairs={{1,0},{2,1},{3,2},{4,3},{5,4},{6,5},{7,6},{8,7},{9,8},{10,9},{11,1... | collective-permute-start | bytes 393224 | tf_op jit(solution)/shard_map/ppermute | solution.py:15
  143.0 5.8 %collective-permute-start.23 = (f32[8,4,256]{2,0,1:T(8,128)S(1)}, f32[8,4,256]{2,0,1:T(8,128)S(1)}, u32[]{:S(2)}, u32[]{:S(2)}) collective-permute-start(f32[8,4,256]{2,0,1:T(8,128)S(1)} %add.124), channel_id=1, source_target_pairs={{0,128},{32,160},{64,192},{96,224},{128,0},{160,32},{192,64},{224,... | collective-permute-start | bytes 98312 | tf_op jit(solution)/shard_map/ppermute | solution.py:81
  148.8 7.3 %collective-permute-start.24 = (f32[8,4,256]{2,0,1:T(8,128)S(1)}, f32[8,4,256]{2,0,1:T(8,128)S(1)}, u32[]{:S(2)}, u32[]{:S(2)}) collective-permute-start(f32[8,4,256]{2,0,1:T(8,128)S(1)} %add.125), channel_id=1, source_target_pairs={{0,256},{32,288},{64,320},{96,352},{128,384},{160,416},{192,448},{... | collective-permute-start | bytes 98312 | tf_op jit(solution)/shard_map/ppermute | solution.py:81
  (6 other events, 41.8 us)

commit v2 on v1

--- a/solution.py
+++ b/solution.py
@@ -6,7 +6,7 @@
 from jax.sharding import PartitionSpec as P
 
 shift_offsets = (1, 2, -1, -2)
-REDUCE = "pp_all"
+REDUCE = "a2a_radix"
 
 
 def from_behind(value, axis, steps):
@@ -80,6 +80,52 @@
         bit = 1 << step
         data = data + lax.ppermute(data, axis, [(source, source ^ bit) for source in range(count)])
     return data
+
+
+def digit_of(axis, stride, size):
+    return (lax.axis_index(axis) // stride) % size
+
+
+def group_pairs(axis, stride, size, shift):
+    count = lax.axis_size(axis)
+    pairs = []
+    for source in range(count):
+        digit = (source // stride) % size
+        pairs.append((source, source + ((digit + shift) % size - digit) * stride))
+    return pairs
+
+
+def group_scatter(data, axis, stride, size, dim):
+    digit = digit_of(axis, stride, size)
+    total = jnp.take(data, digit, axis=dim)
+    for shift in range(1, size):
+        give = jnp.take(data, (digit + shift) % size, axis=dim)
+        total = total + lax.ppermute(give, axis, group_pairs(axis, stride, size, shift))
+    return total
+
+
+def group_sum(data, axis, stride, size):
+    digit = digit_of(axis, stride, size)
+    got = [data] + [lax.ppermute(data, axis, group_pairs(axis, stride, size, shift)) for shift in range(1, size)]
+    stacked = jnp.stack(got)
+    ordered = jnp.take(stacked, (digit - jnp.arange(size)) % size, axis=0)
+    while ordered.shape[0] > 1:
+        ordered = ordered[0::2] + ordered[1::2]
+    return ordered[0]
+
+
+def graph_scatter(partials):
+    graph = lax.axis_size("graph")
+    share = partials.shape[0] // graph
+    data = partials.reshape(graph // 8, 4, 2, share, *partials.shape[1:])
+    data = group_scatter(data, "graph", 1, 2, 2)
+    data = group_scatter(data, "graph", 2, 4, 1)
+    return group_scatter(data, "graph", 8, graph // 8, 0)
+
+
+def scen_sum(data):
+    data = group_sum(data, "scen", 1, 4)
+    return group_sum(data, "scen", 4, lax.axis_size("scen") // 4)
 
 
 def reduce_grads(partials, total_rows):
@@ -111,6 +157,17 @@
         part = lax.psum(halving_scatter(partials, "graph"), "scen")
     elif REDUCE == "pp_all":
         part = doubling_sum(halving_scatter(partials, "graph"), "scen")
+    elif REDUCE == "a2a_radix":
+        pieces = partials.reshape(graph, share, *partials.shape[1:])
+        part = scen_sum(lax.all_to_all(pieces, "graph", 0, 0).sum(0))
+    elif REDUCE == "a2a3":
+        pieces = partials.reshape(graph, share, *partials.shape[1:])
+        part = lax.all_to_all(pieces, "graph", 0, 0).sum(0)
+        flat = lax.all_to_all(part.reshape(scen, -1), "scen", 0, 0).sum(0)
+        flat = lax.all_to_all(jnp.broadcast_to(flat, (scen, *flat.shape)), "scen", 0, 0)
+        part = flat.reshape(part.shape)
+    elif REDUCE == "radix":
+        part = scen_sum(graph_scatter(partials))
     else:
         raise ValueError(REDUCE)
     return part * scale
@@ -144,11 +201,17 @@
     hidden_grad, self2, msg2 = backward(
         hidden, message2, pre2, cotangent, self_weight2, message_weight2, dense, select
     )
+    if REDUCE == "radix_split":
+        early = graph_scatter(jnp.stack((self2, msg2), 1))
     input_grad, self1, msg1 = backward(
         features, message1, pre1, hidden_grad, self_weight1, message_weight1, dense, select
     )
     total_rows = features.shape[0] * bus_count * lax.axis_size("scen") * lax.axis_size("graph")
-    grads = reduce_grads(jnp.stack((self1, msg1, self2, msg2), 1), total_rows)
+    if REDUCE == "radix_split":
+        late = graph_scatter(jnp.stack((self1, msg1), 1))
+        grads = scen_sum(jnp.concatenate((late, early), 1)) * (1.0 / math.sqrt(total_rows))
+    else:
+        grads = reduce_grads(jnp.stack((self1, msg1, self2, msg2), 1), total_rows)
     return (input_grad, grads[:, 0], grads[:, 1], grads[:, 2], grads[:, 3])
 
 

time: 158 us -> 149 us (0.943)
  the two profiles are of different devices: /device:TPU:12 before, /device:TPU:1 now
where the time goes in v2:
time: 149 us; the launch traced here: 147 us
  starting transfers between devices  85.8 us (58%)
  waiting for transfers between devices  40.1 us (27%)
  matrix products  14.5 us (10%)
  local copies, waits for them, and re-layouts  3.9 us (3%)
    ppermute x16, starting transfers between devices, from_behind(): lax.ppermute(value, axis, [(source, source + steps) for source in range(f...  42 us
    ppermute x6, starting transfers between devices, group_sum(): lax.ppermute(data, axis, group_pairs(axis, stride, size, shift))  33.4 us
    all_to_all x1, waiting for transfers between devices, reduce_grads(): part = scen_sum(lax.all_to_all(pieces, 'graph', 0, 0).sum(0))  18.8 us
    ppermute x16, waiting for transfers between devices, from_behind(): lax.ppermute(value, axis, [(source, source + steps) for source in range(f...  17.7 us
    dot_general x18, matrix products, mm(): return jnp.einsum(spec, left, right, preferred_element_type=jnp.float32)  14 us
    all_to_all x1, starting transfers between devices, reduce_grads(): part = scen_sum(lax.all_to_all(pieces, 'graph', 0, 0).sum(0))  10.3 us
    ppermute x6, waiting for transfers between devices, group_sum(): lax.ppermute(data, axis, group_pairs(axis, stride, size, shift))  3.63 us
  transfers between devices with their start and end apart: 23, of which 10 were waited for; matrix products, arithmetic and copies ran while one was open for 5% of the time, Pallas kernels for 0%

profile of v2, /device:TPU:1, one launch (start us, length us, event | category | flops | bytes accessed | tf_op | source)
XLA Modules:
  0.0 147.1 jit_solution(5767065892279463988)
XLA Ops:
  0.7 1.4 fusion.1
  2.8 4.9 %collective-permute-start = (bf16[2,128,256]{2,1,0:T(8,128)(2,1)}, bf16[2,128,256]{2,1,0:T(8,128)(2,1)S(1)}, u32[]{:S(2)}, u32[]{:S(2)}) collective-permute-start(bf16[2,128,256]{2,1,0:T(8,128)(2,1)} %get-tuple-element.23), channel_id=1, source_target_pairs={{0,1},{1,2},{2,3},{3,4},{4,5},{5,6},{6,7},{7,8},{8,9},{9,10},{10,1... | collective-permute-start | bytes 393224 | tf_op jit(solution)/shard_map/ppermute | solution.py:15
  7.7 3.5 %collective-permute-start.1 = (bf16[2,128,256]{2,1,0:T(8,128)(2,1)}, bf16[2,128,256]{2,1,0:T(8,128)(2,1)S(1)}, u32[]{:S(2)}, u32[]{:S(2)}) collective-permute-start(bf16[2,128,256]{2,1,0:T(8,128)(2,1)} %get-tuple-element.22), channel_id=1, source_target_pairs={{0,2},{1,3},{2,4},{3,5},{4,6},{5,7},{6,8},{7,9},{8,10},{9,11},{10,... | collective-permute-start | bytes 393224 | tf_op jit(solution)/shard_map/ppermute | solution.py:15
  11.3 2.9 %collective-permute-start.2 = (bf16[2,128,256]{2,1,0:T(8,128)(2,1)S(1)}, bf16[2,128,256]{2,1,0:T(8,128)(2,1)S(1)}, u32[]{:S(2)}, u32[]{:S(2)}) collective-permute-start(bf16[2,128,256]{2,1,0:T(8,128)(2,1)S(1)} %get-tuple-element.21), channel_id=1, source_target_pairs={{1,0},{2,1},{3,2},{4,3},{5,4},{6,5},{7,6},{8,7},{9,8},{10,9},{11,1... | collective-permute-start | bytes 393224 | tf_op jit(solution)/shard_map/ppermute | solution.py:15
  14.1 1.3 collective-permute-start.3
  18.4 2.9 %collective-permute-done.3 = bf16[2,128,256]{2,1,0:T(8,128)(2,1)S(1)} collective-permute-done((bf16[2,128,256]{2,1,0:T(8,128)(2,1)S(1)}, bf16[2,128,256]{2,1,0:T(8,128)(2,1)S(1)}, u32[]{:S(2)}, u32[]{:S(2)}) %collective-permute-start.3) | collective-permute-done | bytes 131104 | tf_op jit(solution)/shard_map/ppermute | solution.py:15
  23.3 3.2 %collective-permute-start.4 = (bf16[2,128,256]{2,1,0:T(8,128)(2,1)S(1)}, bf16[2,128,256]{2,1,0:T(8,128)(2,1)S(1)}, u32[]{:S(2)}, u32[]{:S(2)}) collective-permute-start(bf16[2,128,256]{2,1,0:T(8,128)(2,1)S(1)} %get-tuple-element.19), channel_id=1, source_target_pairs={{0,1},{1,2},{2,3},{3,4},{4,5},{5,6},{6,7},{7,8},{8,9},{9,10},{10,1... | collective-permute-start | bytes 393224 | tf_op jit(solution)/shard_map/ppermute | solution.py:15
  26.6 2.9 %collective-permute-start.5 = (bf16[2,128,256]{2,1,0:T(8,128)(2,1)S(1)}, bf16[2,128,256]{2,1,0:T(8,128)(2,1)S(1)}, u32[]{:S(2)}, u32[]{:S(2)}) collective-permute-start(bf16[2,128,256]{2,1,0:T(8,128)(2,1)S(1)} %get-tuple-element.18), channel_id=1, source_target_pairs={{0,2},{1,3},{2,4},{3,5},{4,6},{5,7},{6,8},{7,9},{8,10},{9,11},{10,... | collective-permute-start | bytes 393224 | tf_op jit(solution)/shard_map/ppermute | solution.py:15
  29.7 1.9 %collective-permute-start.6 = (bf16[2,128,256]{2,1,0:T(8,128)(2,1)S(1)}, bf16[2,128,256]{2,1,0:T(8,128)(2,1)S(1)}, u32[]{:S(2)}, u32[]{:S(2)}) collective-permute-start(bf16[2,128,256]{2,1,0:T(8,128)(2,1)S(1)} %get-tuple-element.17), channel_id=1, source_target_pairs={{1,0},{2,1},{3,2},{4,3},{5,4},{6,5},{7,6},{8,7},{9,8},{10,9},{11,1... | collective-permute-start | bytes 393224 | tf_op jit(solution)/shard_map/ppermute | solution.py:15
  33.0 5.7 %collective-permute-done.6 = bf16[2,128,256]{2,1,0:T(8,128)(2,1)S(1)} collective-permute-done((bf16[2,128,256]{2,1,0:T(8,128)(2,1)S(1)}, bf16[2,128,256]{2,1,0:T(8,128)(2,1)S(1)}, u32[]{:S(2)}, u32[]{:S(2)}) %collective-permute-start.6) | collective-permute-done | bytes 131104 | tf_op jit(solution)/shard_map/ppermute | solution.py:15
  38.8 2.3 %collective-permute-done.7 = bf16[2,128,256]{2,1,0:T(8,128)(2,1)S(1)} collective-permute-done((bf16[2,128,256]{2,1,0:T(8,128)(2,1)S(1)}, bf16[2,128,256]{2,1,0:T(8,128)(2,1)S(1)}, u32[]{:S(2)}, u32[]{:S(2)}) %collective-permute-start.7) | collective-permute-done | bytes 131104 | tf_op jit(solution)/shard_map/ppermute | solution.py:15
  41.9 2.5 %fusion.61 = (bf16[2,768,256]{2,1,0:T(8,128)(2,1)}, f32[2,768,256]{2,1,0:T(8,128)S(1)}) fusion(bf16[256,768,1]{1,0,2:T(8,128)(2,1)S(1)} %reshape.57, bf16[2,256,256]{2,1,0:T(8,128)(2,1)S(1)} %multiply_convert_fusion, bf16[256,256]{1,0:T(8,128)(2,1)} %param.19), kind=kOutput, calls=%fused_computation.115 | convolution fusion | flops 268959744 | bytes 3145728 | tf_op jit(solution)/shard_map/nm,snd->smd/dot_general | solution.py:33
  46.0 2.9 %collective-permute-start.11 = (bf16[2,128,256]{2,1,0:T(8,128)(2,1)S(1)}, bf16[2,128,256]{2,1,0:T(8,128)(2,1)S(1)}, u32[]{:S(2)}, u32[]{:S(2)}) collective-permute-start(bf16[2,128,256]{2,1,0:T(8,128)(2,1)S(1)} %get-tuple-element.13), channel_id=1, source_target_pairs={{0,2},{1,3},{2,4},{3,5},{4,6},{5,7},{6,8},{7,9},{8,10},{9,11},{10,... | collective-permute-start | bytes 393224 | tf_op jit(solution)/shard_map/ppermute | solution.py:15
  48.9 3.8 %collective-permute-start.10 = (bf16[2,128,256]{2,1,0:T(8,128)(2,1)S(1)}, bf16[2,128,256]{2,1,0:T(8,128)(2,1)S(1)}, u32[]{:S(2)}, u32[]{:S(2)}) collective-permute-start(bf16[2,128,256]{2,1,0:T(8,128)(2,1)S(1)} %get-tuple-element.14), channel_id=1, source_target_pairs={{0,1},{1,2},{2,3},{3,4},{4,5},{5,6},{6,7},{7,8},{8,9},{9,10},{10,1... | collective-permute-start | bytes 393224 | tf_op jit(solution)/shard_map/ppermute | solution.py:15
  54.0 1.9 %collective-permute-start.8 = (bf16[2,128,256]{2,1,0:T(8,128)(2,1)S(1)}, bf16[2,128,256]{2,1,0:T(8,128)(2,1)S(1)}, u32[]{:S(2)}, u32[]{:S(2)}) collective-permute-start(bf16[2,128,256]{2,1,0:T(8,128)(2,1)S(1)} %get-tuple-element.12), channel_id=1, source_target_pairs={{1,0},{2,1},{3,2},{4,3},{5,4},{6,5},{7,6},{8,7},{9,8},{10,9},{11,1... | collective-permute-start | bytes 393224 | tf_op jit(solution)/shard_map/ppermute | solution.py:15
  56.2 5.7 %collective-permute-done.9 = bf16[2,128,256]{2,1,0:T(8,128)(2,1)S(1)} collective-permute-done((bf16[2,128,256]{2,1,0:T(8,128)(2,1)S(1)}, bf16[2,128,256]{2,1,0:T(8,128)(2,1)S(1)}, u32[]{:S(2)}, u32[]{:S(2)}) %collective-permute-start.9) | collective-permute-done | bytes 131104 | tf_op jit(solution)/shard_map/ppermute | solution.py:15
  64.2 10.3 %all-to-all-start = ((f32[32,8,4,256]{3,1,2,0:T(8,128)}), f32[32,8,4,256]{3,1,2,0:T(8,128)S(1)}, u32[]{:S(2)}, u32[]{:S(2)}) async-start(f32[32,8,4,256]{3,1,2,0:T(8,128)} %pad_maximum_fusion), calls=%async_computation | async-start | bytes 2097152 | tf_op jit(solution)/shard_map/all_to_all | solution.py:162
  74.7 1.8 %fusion.64 = (bf16[2,768,256]{2,1,0:T(8,128)(2,1)S(1)}, f32[2,768,256]{2,1,0:T(8,128)}) fusion(bf16[256,768,1]{1,0,2:T(8,128)(2,1)S(1)} %reshape.57, bf16[2,256,256]{2,1,0:T(8,128)(2,1)S(1)} %fusion.9, bf16[256,256]{1,0:T(8,128)(2,1)S(1)} %copy-done.8), kind=kOutput, calls=%fused_computation.116 | convolution fusion | flops 268959744 | bytes 3145728 | tf_op jit(solution)/shard_map/nm,snd->smd/dot_general | solution.py:33
  76.5 3.3 %collective-permute-start.15 = (bf16[2,128,256]{2,1,0:T(8,128)(2,1)S(1)}, bf16[2,128,256]{2,1,0:T(8,128)(2,1)S(1)}, u32[]{:S(2)}, u32[]{:S(2)}) collective-permute-start(bf16[2,128,256]{2,1,0:T(8,128)(2,1)S(1)} %get-tuple-element.9), channel_id=1, source_target_pairs={{0,2},{1,3},{2,4},{3,5},{4,6},{5,7},{6,8},{7,9},{8,10},{9,11},{10,... | collective-permute-start | bytes 393224 | tf_op jit(solution)/shard_map/ppermute | solution.py:15
  79.8 3.6 %collective-permute-start.14 = (bf16[2,128,256]{2,1,0:T(8,128)(2,1)S(1)}, bf16[2,128,256]{2,1,0:T(8,128)(2,1)S(1)}, u32[]{:S(2)}, u32[]{:S(2)}) collective-permute-start(bf16[2,128,256]{2,1,0:T(8,128)(2,1)S(1)} %get-tuple-element.10), channel_id=1, source_target_pairs={{0,1},{1,2},{2,3},{3,4},{4,5},{5,6},{6,7},{7,8},{8,9},{9,10},{10,1... | collective-permute-start | bytes 393224 | tf_op jit(solution)/shard_map/ppermute | solution.py:15
  83.5 1.3 collective-permute-start.13
  84.8 1.9 %collective-permute-start.12 = (bf16[2,128,256]{2,1,0:T(8,128)(2,1)S(1)}, bf16[2,128,256]{2,1,0:T(8,128)(2,1)S(1)}, u32[]{:S(2)}, u32[]{:S(2)}) collective-permute-start(bf16[2,128,256]{2,1,0:T(8,128)(2,1)S(1)} %get-tuple-element.8), channel_id=1, source_target_pairs={{1,0},{2,1},{3,2},{4,3},{5,4},{6,5},{7,6},{8,7},{9,8},{10,9},{11,1... | collective-permute-start | bytes 393224 | tf_op jit(solution)/shard_map/ppermute | solution.py:15
  86.7 1.3 convolution_add_fusion
  88.0 18.8 %all-to-all-done = f32[32,8,4,256]{3,1,2,0:T(8,128)S(1)} async-done(((f32[32,8,4,256]{3,1,2,0:T(8,128)}), f32[32,8,4,256]{3,1,2,0:T(8,128)S(1)}, u32[]{:S(2)}, u32[]{:S(2)}) %all-to-all-start) | async-done | bytes 1048608 | tf_op jit(solution)/shard_map/all_to_all | solution.py:162
  106.8 11.6 %collective-permute-start.18 = (f32[8,4,256]{2,0,1:T(8,128)S(1)}, f32[8,4,256]{2,0,1:T(8,128)S(1)}, u32[]{:S(2)}, u32[]{:S(2)}) collective-permute-start(f32[8,4,256]{2,0,1:T(8,128)S(1)} %reduce_sum.9), channel_id=1, source_target_pairs={{0,96},{32,0},{64,32},{96,64},{128,224},{160,128},{192,160},{224,1... | collective-permute-start | bytes 98312 | tf_op jit(solution)/shard_map/ppermute | solution.py:109
  118.4 5.3 %collective-permute-start.17 = (f32[8,4,256]{2,0,1:T(8,128)S(1)}, f32[8,4,256]{2,0,1:T(8,128)S(1)}, u32[]{:S(2)}, u32[]{:S(2)}) collective-permute-start(f32[8,4,256]{2,0,1:T(8,128)S(1)} %reduce_sum.9), channel_id=1, source_target_pairs={{0,64},{32,96},{64,0},{96,32},{128,192},{160,224},{192,128},{224,1... | collective-permute-start | bytes 98312 | tf_op jit(solution)/shard_map/ppermute | solution.py:109
  123.7 7.3 %collective-permute-start.16 = (f32[8,4,256]{2,0,1:T(8,128)S(1)}, f32[8,4,256]{2,0,1:T(8,128)S(1)}, u32[]{:S(2)}, u32[]{:S(2)}) collective-permute-start(f32[8,4,256]{2,0,1:T(8,128)S(1)} %reduce_sum.9), channel_id=1, source_target_pairs={{0,32},{32,64},{64,96},{96,0},{128,160},{160,192},{192,224},{224,1... | collective-permute-start | bytes 98312 | tf_op jit(solution)/shard_map/ppermute | solution.py:109
  133.1 4.4 %collective-permute-start.21 = (f32[8,4,256]{2,0,1:T(8,128)S(1)}, f32[8,4,256]{2,0,1:T(8,128)S(1)}, u32[]{:S(2)}, u32[]{:S(2)}) collective-permute-start(f32[8,4,256]{2,0,1:T(8,128)S(1)} %fusion.91), channel_id=1, source_target_pairs={{0,384},{32,416},{64,448},{96,480},{128,0},{160,32},{192,64},{224,... | collective-permute-start | bytes 98312 | tf_op jit(solution)/shard_map/ppermute | solution.py:109
  137.5 2.4 %collective-permute-start.20 = (f32[8,4,256]{2,0,1:T(8,128)S(1)}, f32[8,4,256]{2,0,1:T(8,128)S(1)}, u32[]{:S(2)}, u32[]{:S(2)}) collective-permute-start(f32[8,4,256]{2,0,1:T(8,128)S(1)} %fusion.91), channel_id=1, source_target_pairs={{0,256},{32,288},{64,320},{96,352},{128,384},{160,416},{192,448},{... | collective-permute-start | bytes 98312 | tf_op jit(solution)/shard_map/ppermute | solution.py:109
  140.0 2.5 %collective-permute-start.19 = (f32[8,4,256]{2,0,1:T(8,128)S(1)}, f32[8,4,256]{2,0,1:T(8,128)S(1)}, u32[]{:S(2)}, u32[]{:S(2)}) collective-permute-start(f32[8,4,256]{2,0,1:T(8,128)S(1)} %fusion.91), channel_id=1, source_target_pairs={{0,128},{32,160},{64,192},{96,224},{128,256},{160,288},{192,320},{... | collective-permute-start | bytes 98312 | tf_op jit(solution)/shard_map/ppermute | solution.py:109
  142.5 1.5 %collective-permute-done.20 = f32[8,4,256]{2,0,1:T(8,128)S(1)} collective-permute-done((f32[8,4,256]{2,0,1:T(8,128)S(1)}, f32[8,4,256]{2,0,1:T(8,128)S(1)}, u32[]{:S(2)}, u32[]{:S(2)}) %collective-permute-start.20) | collective-permute-done | bytes 32800 | tf_op jit(solution)/shard_map/ppermute | solution.py:109
  144.0 1.8 %collective-permute-done.19 = f32[8,4,256]{2,0,1:T(8,128)S(1)} collective-permute-done((f32[8,4,256]{2,0,1:T(8,128)S(1)}, f32[8,4,256]{2,0,1:T(8,128)S(1)}, u32[]{:S(2)}, u32[]{:S(2)}) %collective-permute-start.19) | collective-permute-done | bytes 32800 | tf_op jit(solution)/shard_map/ppermute | solution.py:109
  (98 shorter events, 16.9 us)
Async XLA Ops:
  0.6 15.1 %copy-start = (bf16[1,2,4,128,128]{4,3,2,1,0:T(8,128)(2,1)S(1)}, bf16[1,2,4,128,128]{4,3,2,1,0:T(8,128)(2,1)}, u32[]{:S(2)}) copy-start(bf16[1,2,4,128,128]{4,3,2,1,0:T(8,128)(2,1)} %param.13) | copy-start | bytes 786436
  0.6 14.8 %copy-start.1 = (bf16[2,256,256]{2,1,0:T(8,128)(2,1)S(1)}, bf16[2,256,256]{2,1,0:T(8,128)(2,1)}, u32[]{:S(2)}) copy-start(bf16[2,256,256]{2,1,0:T(8,128)(2,1)} %param.11) | copy-start | bytes 786436
  0.7 14.8 %copy-start.4 = (bf16[256,256]{1,0:T(8,128)(2,1)S(1)}, bf16[256,256]{1,0:T(8,128)(2,1)}, u32[]{:S(2)}) copy-start(bf16[256,256]{1,0:T(8,128)(2,1)} %param.16) | copy-start | bytes 393220
  0.7 15.0 %copy-start.10 = (s32[1,2,4]{2,1,0:T(2,128)S(1)}, s32[1,2,4]{2,1,0:T(2,128)}, u32[]{:S(2)}) copy-start(s32[1,2,4]{2,1,0:T(2,128)} %param.14) | copy-start | bytes 100
  2.8 14.0 %collective-permute-start = (bf16[2,128,256]{2,1,0:T(8,128)(2,1)}, bf16[2,128,256]{2,1,0:T(8,128)(2,1)S(1)}, u32[]{:S(2)}, u32[]{:S(2)}) collective-permute-start(bf16[2,128,256]{2,1,0:T(8,128)(2,1)} %get-tuple-element.23), channel_id=1, source_target_pairs={{0,1},{1,2},{2,3},{3,4},{4,5},{5,6},{6,7},{7,8},{8,9},{9,10},{10,1... | collective-permute-start | bytes 393224 | tf_op jit(solution)/shard_map/ppermute | solution.py:15
  7.7 9.3 %collective-permute-start.1 = (bf16[2,128,256]{2,1,0:T(8,128)(2,1)}, bf16[2,128,256]{2,1,0:T(8,128)(2,1)S(1)}, u32[]{:S(2)}, u32[]{:S(2)}) collective-permute-start(bf16[2,128,256]{2,1,0:T(8,128)(2,1)} %get-tuple-element.22), channel_id=1, source_target_pairs={{0,2},{1,3},{2,4},{3,5},{4,6},{5,7},{6,8},{7,9},{8,10},{9,11},{10,... | collective-permute-start | bytes 393224 | tf_op jit(solution)/shard_map/ppermute | solution.py:15
  11.3 6.9 %collective-permute-start.2 = (bf16[2,128,256]{2,1,0:T(8,128)(2,1)S(1)}, bf16[2,128,256]{2,1,0:T(8,128)(2,1)S(1)}, u32[]{:S(2)}, u32[]{:S(2)}) collective-permute-start(bf16[2,128,256]{2,1,0:T(8,128)(2,1)S(1)} %get-tuple-element.21), channel_id=1, source_target_pairs={{1,0},{2,1},{3,2},{4,3},{5,4},{6,5},{7,6},{8,7},{9,8},{10,9},{11,1... | collective-permute-start | bytes 393224 | tf_op jit(solution)/shard_map/ppermute | solution.py:15
  14.1 7.1 %collective-permute-start.3 = (bf16[2,128,256]{2,1,0:T(8,128)(2,1)S(1)}, bf16[2,128,256]{2,1,0:T(8,128)(2,1)S(1)}, u32[]{:S(2)}, u32[]{:S(2)}) collective-permute-start(bf16[2,128,256]{2,1,0:T(8,128)(2,1)S(1)} %get-tuple-element.20), channel_id=1, source_target_pairs={{2,0},{3,1},{4,2},{5,3},{6,4},{7,5},{8,6},{9,7},{10,8},{11,9},{12,... | collective-permute-start | bytes 393224 | tf_op jit(solution)/shard_map/ppermute | solution.py:15
  23.3 9.6 %collective-permute-start.4 = (bf16[2,128,256]{2,1,0:T(8,128)(2,1)S(1)}, bf16[2,128,256]{2,1,0:T(8,128)(2,1)S(1)}, u32[]{:S(2)}, u32[]{:S(2)}) collective-permute-start(bf16[2,128,256]{2,1,0:T(8,128)(2,1)S(1)} %get-tuple-element.19), channel_id=1, source_target_pairs={{0,1},{1,2},{2,3},{3,4},{4,5},{5,6},{6,7},{7,8},{8,9},{9,10},{10,1... | collective-permute-start | bytes 393224 | tf_op jit(solution)/shard_map/ppermute | solution.py:15
  26.6 14.9 %copy-start.6 = (bf16[256,256]{1,0:T(8,128)(2,1)S(1)}, bf16[256,256]{1,0:T(8,128)(2,1)}, u32[]{:S(2)}) copy-start(bf16[256,256]{1,0:T(8,128)(2,1)} %param.19) | copy-start | bytes 393220
  26.6 14.9 %copy-start.11 = (bf16[2,256,256]{2,1,0:T(8,128)(2,1)S(1)}, bf16[2,256,256]{2,1,0:T(8,128)(2,1)}, u32[]{:S(2)}) copy-start(bf16[2,256,256]{2,1,0:T(8,128)(2,1)} %param.12) | copy-start | bytes 786436
  26.6 6.4 %collective-permute-start.5 = (bf16[2,128,256]{2,1,0:T(8,128)(2,1)S(1)}, bf16[2,128,256]{2,1,0:T(8,128)(2,1)S(1)}, u32[]{:S(2)}, u32[]{:S(2)}) collective-permute-start(bf16[2,128,256]{2,1,0:T(8,128)(2,1)S(1)} %get-tuple-element.18), channel_id=1, source_target_pairs={{0,2},{1,3},{2,4},{3,5},{4,6},{5,7},{6,8},{7,9},{8,10},{9,11},{10,... | collective-permute-start | bytes 393224 | tf_op jit(solution)/shard_map/ppermute | solution.py:15
  29.7 9.0 %collective-permute-start.6 = (bf16[2,128,256]{2,1,0:T(8,128)(2,1)S(1)}, bf16[2,128,256]{2,1,0:T(8,128)(2,1)S(1)}, u32[]{:S(2)}, u32[]{:S(2)}) collective-permute-start(bf16[2,128,256]{2,1,0:T(8,128)(2,1)S(1)} %get-tuple-element.17), channel_id=1, source_target_pairs={{1,0},{2,1},{3,2},{4,3},{5,4},{6,5},{7,6},{8,7},{9,8},{10,9},{11,1... | collective-permute-start | bytes 393224 | tf_op jit(solution)/shard_map/ppermute | solution.py:15
  31.7 9.4 %collective-permute-start.7 = (bf16[2,128,256]{2,1,0:T(8,128)(2,1)S(1)}, bf16[2,128,256]{2,1,0:T(8,128)(2,1)S(1)}, u32[]{:S(2)}, u32[]{:S(2)}) collective-permute-start(bf16[2,128,256]{2,1,0:T(8,128)(2,1)S(1)} %get-tuple-element.16), channel_id=1, source_target_pairs={{2,0},{3,1},{4,2},{5,3},{6,4},{7,5},{8,6},{9,7},{10,8},{11,9},{12,... | collective-permute-start | bytes 393224 | tf_op jit(solution)/shard_map/ppermute | solution.py:15
  44.7 17.4 %copy-start.12 = (f32[2,256,256]{2,1,0:T(8,128)S(1)}, f32[2,256,256]{2,1,0:T(8,128)}, u32[]{:S(2)}) copy-start(f32[2,256,256]{2,1,0:T(8,128)} %get-tuple-element.28) | copy-start | bytes 1572868
  46.0 10.2 %collective-permute-start.11 = (bf16[2,128,256]{2,1,0:T(8,128)(2,1)S(1)}, bf16[2,128,256]{2,1,0:T(8,128)(2,1)S(1)}, u32[]{:S(2)}, u32[]{:S(2)}) collective-permute-start(bf16[2,128,256]{2,1,0:T(8,128)(2,1)S(1)} %get-tuple-element.13), channel_id=1, source_target_pairs={{0,2},{1,3},{2,4},{3,5},{4,6},{5,7},{6,8},{7,9},{8,10},{9,11},{10,... | collective-permute-start | bytes 393224 | tf_op jit(solution)/shard_map/ppermute | solution.py:15
  48.9 7.3 %collective-permute-start.10 = (bf16[2,128,256]{2,1,0:T(8,128)(2,1)S(1)}, bf16[2,128,256]{2,1,0:T(8,128)(2,1)S(1)}, u32[]{:S(2)}, u32[]{:S(2)}) collective-permute-start(bf16[2,128,256]{2,1,0:T(8,128)(2,1)S(1)} %get-tuple-element.14), channel_id=1, source_target_pairs={{0,1},{1,2},{2,3},{3,4},{4,5},{5,6},{6,7},{7,8},{8,9},{9,10},{10,1... | collective-permute-start | bytes 393224 | tf_op jit(solution)/shard_map/ppermute | solution.py:15
  52.7 9.2 %collective-permute-start.9 = (bf16[2,128,256]{2,1,0:T(8,128)(2,1)S(1)}, bf16[2,128,256]{2,1,0:T(8,128)(2,1)S(1)}, u32[]{:S(2)}, u32[]{:S(2)}) collective-permute-start(bf16[2,128,256]{2,1,0:T(8,128)(2,1)S(1)} %get-tuple-element.15), channel_id=1, source_target_pairs={{2,0},{3,1},{4,2},{5,3},{6,4},{7,5},{8,6},{9,7},{10,8},{11,9},{12,... | collective-permute-start | bytes 393224 | tf_op jit(solution)/shard_map/ppermute | solution.py:15
  54.0 8.0 %collective-permute-start.8 = (bf16[2,128,256]{2,1,0:T(8,128)(2,1)S(1)}, bf16[2,128,256]{2,1,0:T(8,128)(2,1)S(1)}, u32[]{:S(2)}, u32[]{:S(2)}) collective-permute-start(bf16[2,128,256]{2,1,0:T(8,128)(2,1)S(1)} %get-tuple-element.12), channel_id=1, source_target_pairs={{1,0},{2,1},{3,2},{4,3},{5,4},{6,5},{7,6},{8,7},{9,8},{10,9},{11,1... | collective-permute-start | bytes 393224 | tf_op jit(solution)/shard_map/ppermute | solution.py:15
  64.2 10.5 %copy-start.8 = (bf16[256,256]{1,0:T(8,128)(2,1)S(1)}, bf16[256,256]{1,0:T(8,128)(2,1)}, u32[]{:S(2)}) copy-start(bf16[256,256]{1,0:T(8,128)(2,1)} %param.17) | copy-start | bytes 393220
  64.2 42.6 %all-to-all-start = ((f32[32,8,4,256]{3,1,2,0:T(8,128)}), f32[32,8,4,256]{3,1,2,0:T(8,128)S(1)}, u32[]{:S(2)}, u32[]{:S(2)}) async-start(f32[32,8,4,256]{3,1,2,0:T(8,128)} %pad_maximum_fusion), calls=%async_computation | async-start | bytes 2097152 | tf_op jit(solution)/shard_map/all_to_all | solution.py:162
  74.6 12.0 %copy-start.5 = (bf16[256,256]{1,0:T(8,128)(2,1)S(1)}, bf16[256,256]{1,0:T(8,128)(2,1)}, u32[]{:S(2)}) copy-start(bf16[256,256]{1,0:T(8,128)(2,1)} %param.16) | copy-start | bytes 393220
  76.5 41.9 %collective-permute-start.15 = (bf16[2,128,256]{2,1,0:T(8,128)(2,1)S(1)}, bf16[2,128,256]{2,1,0:T(8,128)(2,1)S(1)}, u32[]{:S(2)}, u32[]{:S(2)}) collective-permute-start(bf16[2,128,256]{2,1,0:T(8,128)(2,1)S(1)} %get-tuple-element.9), channel_id=1, source_target_pairs={{0,2},{1,3},{2,4},{3,5},{4,6},{5,7},{6,8},{7,9},{8,10},{9,11},{10,... | collective-permute-start | bytes 393224 | tf_op jit(solution)/shard_map/ppermute | solution.py:15
  79.8 43.9 %collective-permute-start.14 = (bf16[2,128,256]{2,1,0:T(8,128)(2,1)S(1)}, bf16[2,128,256]{2,1,0:T(8,128)(2,1)S(1)}, u32[]{:S(2)}, u32[]{:S(2)}) collective-permute-start(bf16[2,128,256]{2,1,0:T(8,128)(2,1)S(1)} %get-tuple-element.10), channel_id=1, source_target_pairs={{0,1},{1,2},{2,3},{3,4},{4,5},{5,6},{6,7},{7,8},{8,9},{9,10},{10,1... | collective-permute-start | bytes 393224 | tf_op jit(solution)/shard_map/ppermute | solution.py:15
  83.5 47.5 %collective-permute-start.13 = (bf16[2,128,256]{2,1,0:T(8,128)(2,1)S(1)}, bf16[2,128,256]{2,1,0:T(8,128)(2,1)S(1)}, u32[]{:S(2)}, u32[]{:S(2)}) collective-permute-start(bf16[2,128,256]{2,1,0:T(8,128)(2,1)S(1)} %get-tuple-element.11), channel_id=1, source_target_pairs={{2,0},{3,1},{4,2},{5,3},{6,4},{7,5},{8,6},{9,7},{10,8},{11,9},{12,... | collective-permute-start | bytes 393224 | tf_op jit(solution)/shard_map/ppermute | solution.py:15
  84.8 46.2 %collective-permute-start.12 = (bf16[2,128,256]{2,1,0:T(8,128)(2,1)S(1)}, bf16[2,128,256]{2,1,0:T(8,128)(2,1)S(1)}, u32[]{:S(2)}, u32[]{:S(2)}) collective-permute-start(bf16[2,128,256]{2,1,0:T(8,128)(2,1)S(1)} %get-tuple-element.8), channel_id=1, source_target_pairs={{1,0},{2,1},{3,2},{4,3},{5,4},{6,5},{7,6},{8,7},{9,8},{10,9},{11,1... | collective-permute-start | bytes 393224 | tf_op jit(solution)/shard_map/ppermute | solution.py:15
  106.8 25.3 %collective-permute-start.18 = (f32[8,4,256]{2,0,1:T(8,128)S(1)}, f32[8,4,256]{2,0,1:T(8,128)S(1)}, u32[]{:S(2)}, u32[]{:S(2)}) collective-permute-start(f32[8,4,256]{2,0,1:T(8,128)S(1)} %reduce_sum.9), channel_id=1, source_target_pairs={{0,96},{32,0},{64,32},{96,64},{128,224},{160,128},{192,160},{224,1... | collective-permute-start | bytes 98312 | tf_op jit(solution)/shard_map/ppermute | solution.py:109
  118.4 13.7 %collective-permute-start.17 = (f32[8,4,256]{2,0,1:T(8,128)S(1)}, f32[8,4,256]{2,0,1:T(8,128)S(1)}, u32[]{:S(2)}, u32[]{:S(2)}) collective-permute-start(f32[8,4,256]{2,0,1:T(8,128)S(1)} %reduce_sum.9), channel_id=1, source_target_pairs={{0,64},{32,96},{64,0},{96,32},{128,192},{160,224},{192,128},{224,1... | collective-permute-start | bytes 98312 | tf_op jit(solution)/shard_map/ppermute | solution.py:109
  123.7 8.8 %collective-permute-start.16 = (f32[8,4,256]{2,0,1:T(8,128)S(1)}, f32[8,4,256]{2,0,1:T(8,128)S(1)}, u32[]{:S(2)}, u32[]{:S(2)}) collective-permute-start(f32[8,4,256]{2,0,1:T(8,128)S(1)} %reduce_sum.9), channel_id=1, source_target_pairs={{0,32},{32,64},{64,96},{96,0},{128,160},{160,192},{192,224},{224,1... | collective-permute-start | bytes 98312 | tf_op jit(solution)/shard_map/ppermute | solution.py:109
  133.1 9.4 %collective-permute-start.21 = (f32[8,4,256]{2,0,1:T(8,128)S(1)}, f32[8,4,256]{2,0,1:T(8,128)S(1)}, u32[]{:S(2)}, u32[]{:S(2)}) collective-permute-start(f32[8,4,256]{2,0,1:T(8,128)S(1)} %fusion.91), channel_id=1, source_target_pairs={{0,384},{32,416},{64,448},{96,480},{128,0},{160,32},{192,64},{224,... | collective-permute-start | bytes 98312 | tf_op jit(solution)/shard_map/ppermute | solution.py:109
  137.5 6.5 %collective-permute-start.20 = (f32[8,4,256]{2,0,1:T(8,128)S(1)}, f32[8,4,256]{2,0,1:T(8,128)S(1)}, u32[]{:S(2)}, u32[]{:S(2)}) collective-permute-start(f32[8,4,256]{2,0,1:T(8,128)S(1)} %fusion.91), channel_id=1, source_target_pairs={{0,256},{32,288},{64,320},{96,352},{128,384},{160,416},{192,448},{... | collective-permute-start | bytes 98312 | tf_op jit(solution)/shard_map/ppermute | solution.py:109
  140.0 5.9 %collective-permute-start.19 = (f32[8,4,256]{2,0,1:T(8,128)S(1)}, f32[8,4,256]{2,0,1:T(8,128)S(1)}, u32[]{:S(2)}, u32[]{:S(2)}) collective-permute-start(f32[8,4,256]{2,0,1:T(8,128)S(1)} %fusion.91), channel_id=1, source_target_pairs={{0,128},{32,160},{64,192},{96,224},{128,256},{160,288},{192,320},{... | collective-permute-start | bytes 98312 | tf_op jit(solution)/shard_map/ppermute | solution.py:109
  (4 other events, 14.0 us)

commit v3 on v2

--- a/solution.py
+++ b/solution.py
@@ -6,7 +6,7 @@
 from jax.sharding import PartitionSpec as P
 
 shift_offsets = (1, 2, -1, -2)
-REDUCE = "a2a_radix"
+REDUCE = "a2a_split"
 
 
 def from_behind(value, axis, steps):
@@ -126,6 +126,12 @@
 def scen_sum(data):
     data = group_sum(data, "scen", 1, 4)
     return group_sum(data, "scen", 4, lax.axis_size("scen") // 4)
+
+
+def graph_a2a(partials):
+    graph = lax.axis_size("graph")
+    pieces = partials.reshape(graph, partials.shape[0] // graph, *partials.shape[1:])
+    return lax.all_to_all(pieces, "graph", 0, 0).sum(0)
 
 
 def reduce_grads(partials, total_rows):
@@ -166,6 +172,11 @@
         flat = lax.all_to_all(part.reshape(scen, -1), "scen", 0, 0).sum(0)
         flat = lax.all_to_all(jnp.broadcast_to(flat, (scen, *flat.shape)), "scen", 0, 0)
         part = flat.reshape(part.shape)
+    elif REDUCE == "a2a_joint":
+        pieces = partials.reshape(graph * scen, -1)
+        piece = lax.all_to_all(pieces, ("graph", "scen"), 0, 0).sum(0)
+        flat = lax.all_to_all(jnp.broadcast_to(piece, (scen, *piece.shape)), "scen", 0, 0)
+        part = flat.reshape(share, *partials.shape[1:])
     elif REDUCE == "radix":
         part = scen_sum(graph_scatter(partials))
     else:
@@ -203,11 +214,21 @@
     )
     if REDUCE == "radix_split":
         early = graph_scatter(jnp.stack((self2, msg2), 1))
+    if REDUCE == "a2a_split":
+        early = graph_a2a(jnp.stack((self2, msg2), 1))
+    if REDUCE == "a2a_split2":
+        early = scen_sum(graph_a2a(jnp.stack((self2, msg2), 1)))
     input_grad, self1, msg1 = backward(
         features, message1, pre1, hidden_grad, self_weight1, message_weight1, dense, select
     )
     total_rows = features.shape[0] * bus_count * lax.axis_size("scen") * lax.axis_size("graph")
-    if REDUCE == "radix_split":
+    if REDUCE == "a2a_split2":
+        late = scen_sum(graph_a2a(jnp.stack((self1, msg1), 1)))
+        grads = jnp.concatenate((late, early), 1) * (1.0 / math.sqrt(total_rows))
+    elif REDUCE == "a2a_split":
+        late = graph_a2a(jnp.stack((self1, msg1), 1))
+        grads = scen_sum(jnp.concatenate((late, early), 1)) * (1.0 / math.sqrt(total_rows))
+    elif REDUCE == "radix_split":
         late = graph_scatter(jnp.stack((self1, msg1), 1))
         grads = scen_sum(jnp.concatenate((late, early), 1)) * (1.0 / math.sqrt(total_rows))
     else:

time: 149 us -> 148 us (level)
  waiting for transfers between devices: 40.1 us -> 23.8 us
  starting transfers between devices: 85.8 us -> 100 us
  matrix products: 14.5 us -> 11.2 us
  other arithmetic: 1.44 us -> 4.68 us
    all_to_all x1 -> x2, waiting for transfers between devices: 18.8 us -> 7.16 us  [graph_a2a(): return lax.all_to_all(pieces, 'graph', 0, 0).sum(0)]
    all_to_all x1 -> x2, starting transfers between devices: 10.3 us -> 19.5 us  [graph_a2a(): return lax.all_to_all(pieces, 'graph', 0, 0).sum(0)]
    ppermute x16, starting transfers between devices: 42 us -> 49.3 us  [from_behind(): lax.ppermute(value, axis, [(source, source + steps) for source in range(f...]
    ppermute x16, waiting for transfers between devices: 17.7 us -> 11.1 us  [from_behind(): lax.ppermute(value, axis, [(source, source + steps) for source in range(f...]
    dot_general x18, matrix products: 14 us -> 10.8 us  [mm(): return jnp.einsum(spec, left, right, preferred_element_type=jnp.float32)]
    reduce_sum x1 -> x2, other arithmetic: 0.07 us -> 2.18 us  [graph_a2a(): return lax.all_to_all(pieces, 'graph', 0, 0).sum(0)]
    ppermute x6, starting transfers between devices: 33.4 us -> 31.4 us  [group_sum(): lax.ppermute(data, axis, group_pairs(axis, stride, size, shift))]
    ppermute x6, waiting for transfers between devices: 3.63 us -> 5.55 us  [group_sum(): lax.ppermute(data, axis, group_pairs(axis, stride, size, shift))]
  transfers between devices with their start and end apart: 23 -> 24, of which waited for: 10 -> 7; matrix products, arithmetic and copies ran while one was open for 5% -> 8% of each run, Pallas kernels for 0% -> 0%
where the time goes in v3:
time: 148 us; the launch traced here: 146 us
  starting transfers between devices  100 us (68%)
  waiting for transfers between devices  23.8 us (16%)
  matrix products  11.2 us (8%)
  local copies, waits for them, and re-layouts  5.11 us (3%)
  other arithmetic  4.68 us (3%)
  between operations  1.48 us (1%)
    ppermute x16, starting transfers between devices, from_behind(): lax.ppermute(value, axis, [(source, source + steps) for source in range(f...  49.3 us
    ppermute x6, starting transfers between devices, group_sum(): lax.ppermute(data, axis, group_pairs(axis, stride, size, shift))  31.4 us
    all_to_all x2, starting transfers between devices, graph_a2a(): return lax.all_to_all(pieces, 'graph', 0, 0).sum(0)  19.5 us
    ppermute x16, waiting for transfers between devices, from_behind(): lax.ppermute(value, axis, [(source, source + steps) for source in range(f...  11.1 us
    dot_general x18, matrix products, mm(): return jnp.einsum(spec, left, right, preferred_element_type=jnp.float32)  10.8 us
    all_to_all x2, waiting for transfers between devices, graph_a2a(): return lax.all_to_all(pieces, 'graph', 0, 0).sum(0)  7.16 us
    ppermute x6, waiting for transfers between devices, group_sum(): lax.ppermute(data, axis, group_pairs(axis, stride, size, shift))  5.55 us
  transfers between devices with their start and end apart: 24, of which 7 were waited for; matrix products, arithmetic and copies ran while one was open for 8% of the time, Pallas kernels for 0%

profile of v3, /device:TPU:1, one launch (start us, length us, event | category | flops | bytes accessed | tf_op | source)
XLA Modules:
  0.0 146.5 jit_solution(8798394325451140565)
XLA Ops:
  0.7 1.4 fusion.1
  2.8 1.3 collective-permute-start.3
  4.1 8.7 %collective-permute-start.2 = (bf16[2,128,256]{2,1,0:T(8,128)(2,1)S(1)}, bf16[2,128,256]{2,1,0:T(8,128)(2,1)S(1)}, u32[]{:S(2)}, u32[]{:S(2)}) collective-permute-start(bf16[2,128,256]{2,1,0:T(8,128)(2,1)S(1)} %get-tuple-element.21), channel_id=1, source_target_pairs={{1,0},{2,1},{3,2},{4,3},{5,4},{6,5},{7,6},{8,7},{9,8},{10,9},{11,1... | collective-permute-start | bytes 393224 | tf_op jit(solution)/shard_map/ppermute | solution.py:15
  12.8 4.3 %collective-permute-start.1 = (bf16[2,128,256]{2,1,0:T(8,128)(2,1)}, bf16[2,128,256]{2,1,0:T(8,128)(2,1)S(1)}, u32[]{:S(2)}, u32[]{:S(2)}) collective-permute-start(bf16[2,128,256]{2,1,0:T(8,128)(2,1)} %get-tuple-element.22), channel_id=1, source_target_pairs={{0,2},{1,3},{2,4},{3,5},{4,6},{5,7},{6,8},{7,9},{8,10},{9,11},{10,... | collective-permute-start | bytes 393224 | tf_op jit(solution)/shard_map/ppermute | solution.py:15
  17.1 1.9 %collective-permute-start = (bf16[2,128,256]{2,1,0:T(8,128)(2,1)}, bf16[2,128,256]{2,1,0:T(8,128)(2,1)S(1)}, u32[]{:S(2)}, u32[]{:S(2)}) collective-permute-start(bf16[2,128,256]{2,1,0:T(8,128)(2,1)} %get-tuple-element.23), channel_id=1, source_target_pairs={{0,1},{1,2},{2,3},{3,4},{4,5},{5,6},{6,7},{7,8},{8,9},{9,10},{10,1... | collective-permute-start | bytes 393224 | tf_op jit(solution)/shard_map/ppermute | solution.py:15
  20.4 1.7 %collective-permute-done = bf16[2,128,256]{2,1,0:T(8,128)(2,1)S(1)} collective-permute-done((bf16[2,128,256]{2,1,0:T(8,128)(2,1)}, bf16[2,128,256]{2,1,0:T(8,128)(2,1)S(1)}, u32[]{:S(2)}, u32[]{:S(2)}) %collective-permute-start) | collective-permute-done | bytes 131104 | tf_op jit(solution)/shard_map/ppermute | solution.py:15
  24.8 1.3 collective-permute-start.7
  26.1 1.9 %collective-permute-start.6 = (bf16[2,128,256]{2,1,0:T(8,128)(2,1)S(1)}, bf16[2,128,256]{2,1,0:T(8,128)(2,1)S(1)}, u32[]{:S(2)}, u32[]{:S(2)}) collective-permute-start(bf16[2,128,256]{2,1,0:T(8,128)(2,1)S(1)} %get-tuple-element.17), channel_id=1, source_target_pairs={{1,0},{2,1},{3,2},{4,3},{5,4},{6,5},{7,6},{8,7},{9,8},{10,9},{11,1... | collective-permute-start | bytes 393224 | tf_op jit(solution)/shard_map/ppermute | solution.py:15
  28.0 5.0 %collective-permute-start.5 = (bf16[2,128,256]{2,1,0:T(8,128)(2,1)S(1)}, bf16[2,128,256]{2,1,0:T(8,128)(2,1)S(1)}, u32[]{:S(2)}, u32[]{:S(2)}) collective-permute-start(bf16[2,128,256]{2,1,0:T(8,128)(2,1)S(1)} %get-tuple-element.18), channel_id=1, source_target_pairs={{0,2},{1,3},{2,4},{3,5},{4,6},{5,7},{6,8},{7,9},{8,10},{9,11},{10,... | collective-permute-start | bytes 393224 | tf_op jit(solution)/shard_map/ppermute | solution.py:15
  33.0 3.9 %collective-permute-start.4 = (bf16[2,128,256]{2,1,0:T(8,128)(2,1)S(1)}, bf16[2,128,256]{2,1,0:T(8,128)(2,1)S(1)}, u32[]{:S(2)}, u32[]{:S(2)}) collective-permute-start(bf16[2,128,256]{2,1,0:T(8,128)(2,1)S(1)} %get-tuple-element.19), channel_id=1, source_target_pairs={{0,1},{1,2},{2,3},{3,4},{4,5},{5,6},{6,7},{7,8},{8,9},{9,10},{10,1... | collective-permute-start | bytes 393224 | tf_op jit(solution)/shard_map/ppermute | solution.py:15
  37.2 1.7 %collective-permute-done.4 = bf16[2,128,256]{2,1,0:T(8,128)(2,1)S(1)} collective-permute-done((bf16[2,128,256]{2,1,0:T(8,128)(2,1)S(1)}, bf16[2,128,256]{2,1,0:T(8,128)(2,1)S(1)}, u32[]{:S(2)}, u32[]{:S(2)}) %collective-permute-start.4) | collective-permute-done | bytes 131104 | tf_op jit(solution)/shard_map/ppermute | solution.py:15
  41.3 10.6 %all-to-all-start.1 = ((f32[32,8,2,256]{3,1,2,0:T(8,128)}), f32[32,8,2,256]{3,1,2,0:T(8,128)}, u32[]{:S(2)}, u32[]{:S(2)}) async-start(f32[32,8,2,256]{3,1,2,0:T(8,128)} %pad_maximum_fusion.1), calls=%async_computation.1 | async-start | bytes 1048576 | tf_op jit(solution)/shard_map/all_to_all | solution.py:134
  51.9 1.6 %fusion.62 = (bf16[2,768,256]{2,1,0:T(8,128)(2,1)S(1)}, f32[2,768,256]{2,1,0:T(8,128)S(1)}) fusion(bf16[256,768,1]{1,0,2:T(8,128)(2,1)S(1)} %reshape.58, bf16[2,256,256]{2,1,0:T(8,128)(2,1)S(1)} %multiply_convert_fusion, bf16[256,256]{1,0:T(8,128)(2,1)} %param.19), kind=kOutput, calls=%fused_computation.118 | convolution fusion | flops 268959744 | bytes 3145728 | tf_op jit(solution)/shard_map/nm,snd->smd/dot_general | solution.py:33
  53.5 2.4 %collective-permute-start.8 = (bf16[2,128,256]{2,1,0:T(8,128)(2,1)S(1)}, bf16[2,128,256]{2,1,0:T(8,128)(2,1)S(1)}, u32[]{:S(2)}, u32[]{:S(2)}) collective-permute-start(bf16[2,128,256]{2,1,0:T(8,128)(2,1)S(1)} %get-tuple-element.12), channel_id=1, source_target_pairs={{1,0},{2,1},{3,2},{4,3},{5,4},{6,5},{7,6},{8,7},{9,8},{10,9},{11,1... | collective-permute-start | bytes 393224 | tf_op jit(solution)/shard_map/ppermute | solution.py:15
  55.9 3.3 %collective-permute-start.11 = (bf16[2,128,256]{2,1,0:T(8,128)(2,1)S(1)}, bf16[2,128,256]{2,1,0:T(8,128)(2,1)S(1)}, u32[]{:S(2)}, u32[]{:S(2)}) collective-permute-start(bf16[2,128,256]{2,1,0:T(8,128)(2,1)S(1)} %get-tuple-element.13), channel_id=1, source_target_pairs={{0,2},{1,3},{2,4},{3,5},{4,6},{5,7},{6,8},{7,9},{8,10},{9,11},{10,... | collective-permute-start | bytes 393224 | tf_op jit(solution)/shard_map/ppermute | solution.py:15
  59.2 3.5 %collective-permute-start.10 = (bf16[2,128,256]{2,1,0:T(8,128)(2,1)S(1)}, bf16[2,128,256]{2,1,0:T(8,128)(2,1)S(1)}, u32[]{:S(2)}, u32[]{:S(2)}) collective-permute-start(bf16[2,128,256]{2,1,0:T(8,128)(2,1)S(1)} %get-tuple-element.14), channel_id=1, source_target_pairs={{0,1},{1,2},{2,3},{3,4},{4,5},{5,6},{6,7},{7,8},{8,9},{9,10},{10,1... | collective-permute-start | bytes 393224 | tf_op jit(solution)/shard_map/ppermute | solution.py:15
  62.8 1.3 collective-permute-start.9
  65.3 7.6 %collective-permute-done.9 = bf16[2,128,256]{2,1,0:T(8,128)(2,1)S(1)} collective-permute-done((bf16[2,128,256]{2,1,0:T(8,128)(2,1)S(1)}, bf16[2,128,256]{2,1,0:T(8,128)(2,1)S(1)}, u32[]{:S(2)}, u32[]{:S(2)}) %collective-permute-start.9) | collective-permute-done | bytes 131104 | tf_op jit(solution)/shard_map/ppermute | solution.py:15
  75.2 8.8 %all-to-all-start = ((f32[32,8,2,256]{3,1,2,0:T(8,128)}), f32[32,8,2,256]{3,1,2,0:T(8,128)}, u32[]{:S(2)}, u32[]{:S(2)}) async-start(f32[32,8,2,256]{3,1,2,0:T(8,128)} %pad_maximum_fusion), calls=%async_computation | async-start | bytes 1048576 | tf_op jit(solution)/shard_map/all_to_all | solution.py:134
  86.2 2.2 %collective-permute-start.12 = (bf16[2,128,256]{2,1,0:T(8,128)(2,1)}, bf16[2,128,256]{2,1,0:T(8,128)(2,1)S(1)}, u32[]{:S(2)}, u32[]{:S(2)}) collective-permute-start(bf16[2,128,256]{2,1,0:T(8,128)(2,1)} %get-tuple-element.8), channel_id=1, source_target_pairs={{1,0},{2,1},{3,2},{4,3},{5,4},{6,5},{7,6},{8,7},{9,8},{10,9},{11,1... | collective-permute-start | bytes 393224 | tf_op jit(solution)/shard_map/ppermute | solution.py:15
  88.4 3.4 %collective-permute-start.15 = (bf16[2,128,256]{2,1,0:T(8,128)(2,1)}, bf16[2,128,256]{2,1,0:T(8,128)(2,1)S(1)}, u32[]{:S(2)}, u32[]{:S(2)}) collective-permute-start(bf16[2,128,256]{2,1,0:T(8,128)(2,1)} %get-tuple-element.9), channel_id=1, source_target_pairs={{0,2},{1,3},{2,4},{3,5},{4,6},{5,7},{6,8},{7,9},{8,10},{9,11},{10,... | collective-permute-start | bytes 393224 | tf_op jit(solution)/shard_map/ppermute | solution.py:15
  91.7 3.5 %collective-permute-start.14 = (bf16[2,128,256]{2,1,0:T(8,128)(2,1)}, bf16[2,128,256]{2,1,0:T(8,128)(2,1)S(1)}, u32[]{:S(2)}, u32[]{:S(2)}) collective-permute-start(bf16[2,128,256]{2,1,0:T(8,128)(2,1)} %get-tuple-element.10), channel_id=1, source_target_pairs={{0,1},{1,2},{2,3},{3,4},{4,5},{5,6},{6,7},{7,8},{8,9},{9,10},{10,1... | collective-permute-start | bytes 393224 | tf_op jit(solution)/shard_map/ppermute | solution.py:15
  95.3 1.3 collective-permute-start.13
  97.9 7.2 %all-to-all-done = f32[32,8,2,256]{3,1,2,0:T(8,128)} async-done(((f32[32,8,2,256]{3,1,2,0:T(8,128)}), f32[32,8,2,256]{3,1,2,0:T(8,128)}, u32[]{:S(2)}, u32[]{:S(2)}) %all-to-all-start) | async-done | bytes 524320 | tf_op jit(solution)/shard_map/all_to_all | solution.py:134
  106.2 12.9 %collective-permute-start.17 = (f32[8,4,256]{2,0,1:T(8,128)S(1)}, f32[8,4,256]{2,0,1:T(8,128)S(1)}, u32[]{:S(2)}, u32[]{:S(2)}) collective-permute-start(f32[8,4,256]{2,0,1:T(8,128)S(1)} %get-tuple-element.29), channel_id=1, source_target_pairs={{0,64},{32,96},{64,0},{96,32},{128,192},{160,224},{192,128},{224,1... | collective-permute-start | bytes 98312 | tf_op jit(solution)/shard_map/ppermute | solution.py:109
  119.1 4.0 %collective-permute-start.16 = (f32[8,4,256]{2,0,1:T(8,128)S(1)}, f32[8,4,256]{2,0,1:T(8,128)S(1)}, u32[]{:S(2)}, u32[]{:S(2)}) collective-permute-start(f32[8,4,256]{2,0,1:T(8,128)S(1)} %get-tuple-element.29), channel_id=1, source_target_pairs={{0,32},{32,64},{64,96},{96,0},{128,160},{160,192},{192,224},{224,1... | collective-permute-start | bytes 98312 | tf_op jit(solution)/shard_map/ppermute | solution.py:109
  123.2 5.2 %collective-permute-start.18 = (f32[8,4,256]{2,0,1:T(8,128)S(1)}, f32[8,4,256]{2,0,1:T(8,128)S(1)}, u32[]{:S(2)}, u32[]{:S(2)}) collective-permute-start(f32[8,4,256]{2,0,1:T(8,128)S(1)} %get-tuple-element.29), channel_id=1, source_target_pairs={{0,96},{32,0},{64,32},{96,64},{128,224},{160,128},{192,160},{224,1... | collective-permute-start | bytes 98312 | tf_op jit(solution)/shard_map/ppermute | solution.py:109
  129.5 2.2 %collective-permute-done.18 = f32[8,4,256]{2,0,1:T(8,128)S(1)} collective-permute-done((f32[8,4,256]{2,0,1:T(8,128)S(1)}, f32[8,4,256]{2,0,1:T(8,128)S(1)}, u32[]{:S(2)}, u32[]{:S(2)}) %collective-permute-start.18) | collective-permute-done | bytes 32800 | tf_op jit(solution)/shard_map/ppermute | solution.py:109
  132.4 4.4 %collective-permute-start.21 = (f32[8,4,256]{2,0,1:T(8,128)S(1)}, f32[8,4,256]{2,0,1:T(8,128)S(1)}, u32[]{:S(2)}, u32[]{:S(2)}) collective-permute-start(f32[8,4,256]{2,0,1:T(8,128)S(1)} %fusion.92), channel_id=1, source_target_pairs={{0,384},{32,416},{64,448},{96,480},{128,0},{160,32},{192,64},{224,... | collective-permute-start | bytes 98312 | tf_op jit(solution)/shard_map/ppermute | solution.py:109
  136.8 2.4 %collective-permute-start.20 = (f32[8,4,256]{2,0,1:T(8,128)S(1)}, f32[8,4,256]{2,0,1:T(8,128)S(1)}, u32[]{:S(2)}, u32[]{:S(2)}) collective-permute-start(f32[8,4,256]{2,0,1:T(8,128)S(1)} %fusion.92), channel_id=1, source_target_pairs={{0,256},{32,288},{64,320},{96,352},{128,384},{160,416},{192,448},{... | collective-permute-start | bytes 98312 | tf_op jit(solution)/shard_map/ppermute | solution.py:109
  139.3 2.5 %collective-permute-start.19 = (f32[8,4,256]{2,0,1:T(8,128)S(1)}, f32[8,4,256]{2,0,1:T(8,128)S(1)}, u32[]{:S(2)}, u32[]{:S(2)}) collective-permute-start(f32[8,4,256]{2,0,1:T(8,128)S(1)} %fusion.92), channel_id=1, source_target_pairs={{0,128},{32,160},{64,192},{96,224},{128,256},{160,288},{192,320},{... | collective-permute-start | bytes 98312 | tf_op jit(solution)/shard_map/ppermute | solution.py:109
  143.0 2.1 %collective-permute-done.19 = f32[8,4,256]{2,0,1:T(8,128)S(1)} collective-permute-done((f32[8,4,256]{2,0,1:T(8,128)S(1)}, f32[8,4,256]{2,0,1:T(8,128)S(1)}, u32[]{:S(2)}, u32[]{:S(2)}) %collective-permute-start.19) | collective-permute-done | bytes 32800 | tf_op jit(solution)/shard_map/ppermute | solution.py:109
  (107 shorter events, 19.3 us)
Async XLA Ops:
  0.6 18.7 %copy-start = (bf16[1,2,4,128,128]{4,3,2,1,0:T(8,128)(2,1)S(1)}, bf16[1,2,4,128,128]{4,3,2,1,0:T(8,128)(2,1)}, u32[]{:S(2)}) copy-start(bf16[1,2,4,128,128]{4,3,2,1,0:T(8,128)(2,1)} %param.13) | copy-start | bytes 786436
  0.6 18.4 %copy-start.1 = (bf16[2,256,256]{2,1,0:T(8,128)(2,1)S(1)}, bf16[2,256,256]{2,1,0:T(8,128)(2,1)}, u32[]{:S(2)}) copy-start(bf16[2,256,256]{2,1,0:T(8,128)(2,1)} %param.11) | copy-start | bytes 786436
  0.7 18.4 %copy-start.5 = (bf16[256,256]{1,0:T(8,128)(2,1)S(1)}, bf16[256,256]{1,0:T(8,128)(2,1)}, u32[]{:S(2)}) copy-start(bf16[256,256]{1,0:T(8,128)(2,1)} %param.16) | copy-start | bytes 393220
  0.7 18.6 %copy-start.11 = (s32[1,2,4]{2,1,0:T(2,128)S(1)}, s32[1,2,4]{2,1,0:T(2,128)}, u32[]{:S(2)}) copy-start(s32[1,2,4]{2,1,0:T(2,128)} %param.14) | copy-start | bytes 100
  2.8 19.9 %collective-permute-start.3 = (bf16[2,128,256]{2,1,0:T(8,128)(2,1)S(1)}, bf16[2,128,256]{2,1,0:T(8,128)(2,1)S(1)}, u32[]{:S(2)}, u32[]{:S(2)}) collective-permute-start(bf16[2,128,256]{2,1,0:T(8,128)(2,1)S(1)} %get-tuple-element.20), channel_id=1, source_target_pairs={{2,0},{3,1},{4,2},{5,3},{6,4},{7,5},{8,6},{9,7},{10,8},{11,9},{12,... | collective-permute-start | bytes 393224 | tf_op jit(solution)/shard_map/ppermute | solution.py:15
  4.1 18.4 %collective-permute-start.2 = (bf16[2,128,256]{2,1,0:T(8,128)(2,1)S(1)}, bf16[2,128,256]{2,1,0:T(8,128)(2,1)S(1)}, u32[]{:S(2)}, u32[]{:S(2)}) collective-permute-start(bf16[2,128,256]{2,1,0:T(8,128)(2,1)S(1)} %get-tuple-element.21), channel_id=1, source_target_pairs={{1,0},{2,1},{3,2},{4,3},{5,4},{6,5},{7,6},{8,7},{9,8},{10,9},{11,1... | collective-permute-start | bytes 393224 | tf_op jit(solution)/shard_map/ppermute | solution.py:15
  12.8 9.5 %collective-permute-start.1 = (bf16[2,128,256]{2,1,0:T(8,128)(2,1)}, bf16[2,128,256]{2,1,0:T(8,128)(2,1)S(1)}, u32[]{:S(2)}, u32[]{:S(2)}) collective-permute-start(bf16[2,128,256]{2,1,0:T(8,128)(2,1)} %get-tuple-element.22), channel_id=1, source_target_pairs={{0,2},{1,3},{2,4},{3,5},{4,6},{5,7},{6,8},{7,9},{8,10},{9,11},{10,... | collective-permute-start | bytes 393224 | tf_op jit(solution)/shard_map/ppermute | solution.py:15
  17.1 5.0 %collective-permute-start = (bf16[2,128,256]{2,1,0:T(8,128)(2,1)}, bf16[2,128,256]{2,1,0:T(8,128)(2,1)S(1)}, u32[]{:S(2)}, u32[]{:S(2)}) collective-permute-start(bf16[2,128,256]{2,1,0:T(8,128)(2,1)} %get-tuple-element.23), channel_id=1, source_target_pairs={{0,1},{1,2},{2,3},{3,4},{4,5},{5,6},{6,7},{7,8},{8,9},{9,10},{10,1... | collective-permute-start | bytes 393224 | tf_op jit(solution)/shard_map/ppermute | solution.py:15
  24.4 12.6 %copy-start.4 = (bf16[256,256]{1,0:T(8,128)(2,1)S(1)}, bf16[256,256]{1,0:T(8,128)(2,1)}, u32[]{:S(2)}) copy-start(bf16[256,256]{1,0:T(8,128)(2,1)} %param.18) | copy-start | bytes 393220
  24.8 14.2 %collective-permute-start.7 = (bf16[2,128,256]{2,1,0:T(8,128)(2,1)S(1)}, bf16[2,128,256]{2,1,0:T(8,128)(2,1)S(1)}, u32[]{:S(2)}, u32[]{:S(2)}) collective-permute-start(bf16[2,128,256]{2,1,0:T(8,128)(2,1)S(1)} %get-tuple-element.16), channel_id=1, source_target_pairs={{2,0},{3,1},{4,2},{5,3},{6,4},{7,5},{8,6},{9,7},{10,8},{11,9},{12,... | collective-permute-start | bytes 393224 | tf_op jit(solution)/shard_map/ppermute | solution.py:15
  26.1 12.9 %collective-permute-start.6 = (bf16[2,128,256]{2,1,0:T(8,128)(2,1)S(1)}, bf16[2,128,256]{2,1,0:T(8,128)(2,1)S(1)}, u32[]{:S(2)}, u32[]{:S(2)}) collective-permute-start(bf16[2,128,256]{2,1,0:T(8,128)(2,1)S(1)} %get-tuple-element.17), channel_id=1, source_target_pairs={{1,0},{2,1},{3,2},{4,3},{5,4},{6,5},{7,6},{8,7},{9,8},{10,9},{11,1... | collective-permute-start | bytes 393224 | tf_op jit(solution)/shard_map/ppermute | solution.py:15
  28.0 10.9 %collective-permute-start.5 = (bf16[2,128,256]{2,1,0:T(8,128)(2,1)S(1)}, bf16[2,128,256]{2,1,0:T(8,128)(2,1)S(1)}, u32[]{:S(2)}, u32[]{:S(2)}) collective-permute-start(bf16[2,128,256]{2,1,0:T(8,128)(2,1)S(1)} %get-tuple-element.18), channel_id=1, source_target_pairs={{0,2},{1,3},{2,4},{3,5},{4,6},{5,7},{6,8},{7,9},{8,10},{9,11},{10,... | collective-permute-start | bytes 393224 | tf_op jit(solution)/shard_map/ppermute | solution.py:15
  33.0 5.9 %collective-permute-start.4 = (bf16[2,128,256]{2,1,0:T(8,128)(2,1)S(1)}, bf16[2,128,256]{2,1,0:T(8,128)(2,1)S(1)}, u32[]{:S(2)}, u32[]{:S(2)}) collective-permute-start(bf16[2,128,256]{2,1,0:T(8,128)(2,1)S(1)} %get-tuple-element.19), channel_id=1, source_target_pairs={{0,1},{1,2},{2,3},{3,4},{4,5},{5,6},{6,7},{7,8},{8,9},{9,10},{10,1... | collective-permute-start | bytes 393224 | tf_op jit(solution)/shard_map/ppermute | solution.py:15
  41.3 34.0 %all-to-all-start.1 = ((f32[32,8,2,256]{3,1,2,0:T(8,128)}), f32[32,8,2,256]{3,1,2,0:T(8,128)}, u32[]{:S(2)}, u32[]{:S(2)}) async-start(f32[32,8,2,256]{3,1,2,0:T(8,128)} %pad_maximum_fusion.1), calls=%async_computation.1 | async-start | bytes 1048576 | tf_op jit(solution)/shard_map/all_to_all | solution.py:134
  53.5 19.4 %copy-start.14 = (f32[2,256,256]{2,1,0:T(8,128)S(1)}, f32[2,256,256]{2,1,0:T(8,128)}, u32[]{:S(2)}) copy-start(f32[2,256,256]{2,1,0:T(8,128)} %get-tuple-element.30) | copy-start | bytes 1572868
  53.5 11.7 %collective-permute-start.8 = (bf16[2,128,256]{2,1,0:T(8,128)(2,1)S(1)}, bf16[2,128,256]{2,1,0:T(8,128)(2,1)S(1)}, u32[]{:S(2)}, u32[]{:S(2)}) collective-permute-start(bf16[2,128,256]{2,1,0:T(8,128)(2,1)S(1)} %get-tuple-element.12), channel_id=1, source_target_pairs={{1,0},{2,1},{3,2},{4,3},{5,4},{6,5},{7,6},{8,7},{9,8},{10,9},{11,1... | collective-permute-start | bytes 393224 | tf_op jit(solution)/shard_map/ppermute | solution.py:15
  55.9 9.4 %collective-permute-start.11 = (bf16[2,128,256]{2,1,0:T(8,128)(2,1)S(1)}, bf16[2,128,256]{2,1,0:T(8,128)(2,1)S(1)}, u32[]{:S(2)}, u32[]{:S(2)}) collective-permute-start(bf16[2,128,256]{2,1,0:T(8,128)(2,1)S(1)} %get-tuple-element.13), channel_id=1, source_target_pairs={{0,2},{1,3},{2,4},{3,5},{4,6},{5,7},{6,8},{7,9},{8,10},{9,11},{10,... | collective-permute-start | bytes 393224 | tf_op jit(solution)/shard_map/ppermute | solution.py:15
  59.2 6.0 %collective-permute-start.10 = (bf16[2,128,256]{2,1,0:T(8,128)(2,1)S(1)}, bf16[2,128,256]{2,1,0:T(8,128)(2,1)S(1)}, u32[]{:S(2)}, u32[]{:S(2)}) collective-permute-start(bf16[2,128,256]{2,1,0:T(8,128)(2,1)S(1)} %get-tuple-element.14), channel_id=1, source_target_pairs={{0,1},{1,2},{2,3},{3,4},{4,5},{5,6},{6,7},{7,8},{8,9},{9,10},{10,1... | collective-permute-start | bytes 393224 | tf_op jit(solution)/shard_map/ppermute | solution.py:15
  62.8 10.1 %collective-permute-start.9 = (bf16[2,128,256]{2,1,0:T(8,128)(2,1)S(1)}, bf16[2,128,256]{2,1,0:T(8,128)(2,1)S(1)}, u32[]{:S(2)}, u32[]{:S(2)}) collective-permute-start(bf16[2,128,256]{2,1,0:T(8,128)(2,1)S(1)} %get-tuple-element.15), channel_id=1, source_target_pairs={{2,0},{3,1},{4,2},{5,3},{6,4},{7,5},{8,6},{9,7},{10,8},{11,9},{12,... | collective-permute-start | bytes 393224 | tf_op jit(solution)/shard_map/ppermute | solution.py:15
  75.2 29.9 %all-to-all-start = ((f32[32,8,2,256]{3,1,2,0:T(8,128)}), f32[32,8,2,256]{3,1,2,0:T(8,128)}, u32[]{:S(2)}, u32[]{:S(2)}) async-start(f32[32,8,2,256]{3,1,2,0:T(8,128)} %pad_maximum_fusion), calls=%async_computation | async-start | bytes 1048576 | tf_op jit(solution)/shard_map/all_to_all | solution.py:134
  84.7 11.9 %copy-start.6 = (bf16[256,256]{1,0:T(8,128)(2,1)S(1)}, bf16[256,256]{1,0:T(8,128)(2,1)}, u32[]{:S(2)}) copy-start(bf16[256,256]{1,0:T(8,128)(2,1)} %param.16) | copy-start | bytes 393220
  86.2 33.0 %collective-permute-start.12 = (bf16[2,128,256]{2,1,0:T(8,128)(2,1)}, bf16[2,128,256]{2,1,0:T(8,128)(2,1)S(1)}, u32[]{:S(2)}, u32[]{:S(2)}) collective-permute-start(bf16[2,128,256]{2,1,0:T(8,128)(2,1)} %get-tuple-element.8), channel_id=1, source_target_pairs={{1,0},{2,1},{3,2},{4,3},{5,4},{6,5},{7,6},{8,7},{9,8},{10,9},{11,1... | collective-permute-start | bytes 393224 | tf_op jit(solution)/shard_map/ppermute | solution.py:15
  88.4 34.8 %collective-permute-start.15 = (bf16[2,128,256]{2,1,0:T(8,128)(2,1)}, bf16[2,128,256]{2,1,0:T(8,128)(2,1)S(1)}, u32[]{:S(2)}, u32[]{:S(2)}) collective-permute-start(bf16[2,128,256]{2,1,0:T(8,128)(2,1)} %get-tuple-element.9), channel_id=1, source_target_pairs={{0,2},{1,3},{2,4},{3,5},{4,6},{5,7},{6,8},{7,9},{8,10},{9,11},{10,... | collective-permute-start | bytes 393224 | tf_op jit(solution)/shard_map/ppermute | solution.py:15
  91.7 36.6 %collective-permute-start.14 = (bf16[2,128,256]{2,1,0:T(8,128)(2,1)}, bf16[2,128,256]{2,1,0:T(8,128)(2,1)S(1)}, u32[]{:S(2)}, u32[]{:S(2)}) collective-permute-start(bf16[2,128,256]{2,1,0:T(8,128)(2,1)} %get-tuple-element.10), channel_id=1, source_target_pairs={{0,1},{1,2},{2,3},{3,4},{4,5},{5,6},{6,7},{7,8},{8,9},{9,10},{10,1... | collective-permute-start | bytes 393224 | tf_op jit(solution)/shard_map/ppermute | solution.py:15
  95.3 33.1 %collective-permute-start.13 = (bf16[2,128,256]{2,1,0:T(8,128)(2,1)}, bf16[2,128,256]{2,1,0:T(8,128)(2,1)S(1)}, u32[]{:S(2)}, u32[]{:S(2)}) collective-permute-start(bf16[2,128,256]{2,1,0:T(8,128)(2,1)} %get-tuple-element.11), channel_id=1, source_target_pairs={{2,0},{3,1},{4,2},{5,3},{6,4},{7,5},{8,6},{9,7},{10,8},{11,9},{12,... | collective-permute-start | bytes 393224 | tf_op jit(solution)/shard_map/ppermute | solution.py:15
  106.2 26.1 %copy-start.12 = (pred[4]{0:T(512)(128)(4,1)S(1)}, pred[4]{0:T(512)(128)(4,1)}, u32[]{:S(2)}) copy-start(pred[4]{0:T(512)(128)(4,1)} %compare_and_fusion.1) | copy-start | bytes 16
  106.2 23.3 %collective-permute-start.17 = (f32[8,4,256]{2,0,1:T(8,128)S(1)}, f32[8,4,256]{2,0,1:T(8,128)S(1)}, u32[]{:S(2)}, u32[]{:S(2)}) collective-permute-start(f32[8,4,256]{2,0,1:T(8,128)S(1)} %get-tuple-element.29), channel_id=1, source_target_pairs={{0,64},{32,96},{64,0},{96,32},{128,192},{160,224},{192,128},{224,1... | collective-permute-start | bytes 98312 | tf_op jit(solution)/shard_map/ppermute | solution.py:109
  119.1 10.4 %collective-permute-start.16 = (f32[8,4,256]{2,0,1:T(8,128)S(1)}, f32[8,4,256]{2,0,1:T(8,128)S(1)}, u32[]{:S(2)}, u32[]{:S(2)}) collective-permute-start(f32[8,4,256]{2,0,1:T(8,128)S(1)} %get-tuple-element.29), channel_id=1, source_target_pairs={{0,32},{32,64},{64,96},{96,0},{128,160},{160,192},{192,224},{224,1... | collective-permute-start | bytes 98312 | tf_op jit(solution)/shard_map/ppermute | solution.py:109
  123.2 8.6 %collective-permute-start.18 = (f32[8,4,256]{2,0,1:T(8,128)S(1)}, f32[8,4,256]{2,0,1:T(8,128)S(1)}, u32[]{:S(2)}, u32[]{:S(2)}) collective-permute-start(f32[8,4,256]{2,0,1:T(8,128)S(1)} %get-tuple-element.29), channel_id=1, source_target_pairs={{0,96},{32,0},{64,32},{96,64},{128,224},{160,128},{192,160},{224,1... | collective-permute-start | bytes 98312 | tf_op jit(solution)/shard_map/ppermute | solution.py:109
  132.4 9.4 %collective-permute-start.21 = (f32[8,4,256]{2,0,1:T(8,128)S(1)}, f32[8,4,256]{2,0,1:T(8,128)S(1)}, u32[]{:S(2)}, u32[]{:S(2)}) collective-permute-start(f32[8,4,256]{2,0,1:T(8,128)S(1)} %fusion.92), channel_id=1, source_target_pairs={{0,384},{32,416},{64,448},{96,480},{128,0},{160,32},{192,64},{224,... | collective-permute-start | bytes 98312 | tf_op jit(solution)/shard_map/ppermute | solution.py:109
  136.8 6.2 %collective-permute-start.20 = (f32[8,4,256]{2,0,1:T(8,128)S(1)}, f32[8,4,256]{2,0,1:T(8,128)S(1)}, u32[]{:S(2)}, u32[]{:S(2)}) collective-permute-start(f32[8,4,256]{2,0,1:T(8,128)S(1)} %fusion.92), channel_id=1, source_target_pairs={{0,256},{32,288},{64,320},{96,352},{128,384},{160,416},{192,448},{... | collective-permute-start | bytes 98312 | tf_op jit(solution)/shard_map/ppermute | solution.py:109
  139.3 5.9 %collective-permute-start.19 = (f32[8,4,256]{2,0,1:T(8,128)S(1)}, f32[8,4,256]{2,0,1:T(8,128)S(1)}, u32[]{:S(2)}, u32[]{:S(2)}) collective-permute-start(f32[8,4,256]{2,0,1:T(8,128)S(1)} %fusion.92), channel_id=1, source_target_pairs={{0,128},{32,160},{64,192},{96,224},{128,256},{160,288},{192,320},{... | collective-permute-start | bytes 98312 | tf_op jit(solution)/shard_map/ppermute | solution.py:109
  (7 other events, 27.3 us)

commit v4 on v3

--- a/solution.py
+++ b/solution.py
@@ -7,6 +7,8 @@
 
 shift_offsets = (1, 2, -1, -2)
 REDUCE = "a2a_split"
+SCEN = "x_first"
+HOLD = False
 
 
 def from_behind(value, axis, steps):
@@ -52,6 +54,8 @@
     accum = accum + tile_grad[:, :bus_count]
     halo_grad = tile_grad[:, bus_count:].astype(jnp.bfloat16)
     returned = pass_blocks(halo_grad, -1)
+    if HOLD:
+        (self_sum, message_sum), returned = lax.optimization_barrier(((self_sum, message_sum), returned))
     accum = accum + mm(select, returned, "mn,smd->snd")
     return accum.astype(jnp.bfloat16), self_sum, message_sum
 
@@ -124,6 +128,11 @@
 
 
 def scen_sum(data):
+    if SCEN == "doubling":
+        return doubling_sum(data, "scen")
+    if SCEN == "x_first":
+        data = group_sum(data, "scen", 4, lax.axis_size("scen") // 4)
+        return group_sum(data, "scen", 1, 4)
     data = group_sum(data, "scen", 1, 4)
     return group_sum(data, "scen", 4, lax.axis_size("scen") // 4)
 

time: 148 us -> 147 us (level)
  waiting for transfers between devices: 23.8 us -> 21.1 us
  starting transfers between devices: 100 us -> 102 us
    ppermute x6, waiting for transfers between devices: 5.55 us -> 2.91 us  [group_sum(): lax.ppermute(data, axis, group_pairs(axis, stride, size, shift))]
    ppermute x6, starting transfers between devices: 31.4 us -> 33.2 us  [group_sum(): lax.ppermute(data, axis, group_pairs(axis, stride, size, shift))]
  transfers between devices with their start and end apart: 24 -> 24, of which waited for: 7 -> 6; matrix products, arithmetic and copies ran while one was open for 8% -> 8% of each run, Pallas kernels for 0% -> 0%
where the time goes in v4:
time: 147 us; the launch traced here: 146 us
  starting transfers between devices  102 us (69%)
  waiting for transfers between devices  21.1 us (14%)
  matrix products  11.2 us (8%)
  local copies, waits for them, and re-layouts  5.11 us (3%)
  other arithmetic  4.68 us (3%)
  between operations  1.49 us (1%)
    ppermute x16, starting transfers between devices, from_behind(): lax.ppermute(value, axis, [(source, source + steps) for source in range(f...  49.3 us
    ppermute x6, starting transfers between devices, group_sum(): lax.ppermute(data, axis, group_pairs(axis, stride, size, shift))  33.2 us
    all_to_all x2, starting transfers between devices, graph_a2a(): return lax.all_to_all(pieces, 'graph', 0, 0).sum(0)  19.5 us
    ppermute x16, waiting for transfers between devices, from_behind(): lax.ppermute(value, axis, [(source, source + steps) for source in range(f...  11.1 us
    dot_general x18, matrix products, mm(): return jnp.einsum(spec, left, right, preferred_element_type=jnp.float32)  10.8 us
    all_to_all x2, waiting for transfers between devices, graph_a2a(): return lax.all_to_all(pieces, 'graph', 0, 0).sum(0)  7.16 us
  transfers between devices with their start and end apart: 24, of which 6 were waited for; matrix products, arithmetic and copies ran while one was open for 8% of the time, Pallas kernels for 0%

profile of v4, /device:TPU:1, one launch (start us, length us, event | category | flops | bytes accessed | tf_op | source)
XLA Modules:
  0.0 145.6 jit_solution(3754472664964120818)
XLA Ops:
  0.7 1.4 fusion.1
  2.8 1.3 collective-permute-start.3
  4.1 8.7 %collective-permute-start.2 = (bf16[2,128,256]{2,1,0:T(8,128)(2,1)S(1)}, bf16[2,128,256]{2,1,0:T(8,128)(2,1)S(1)}, u32[]{:S(2)}, u32[]{:S(2)}) collective-permute-start(bf16[2,128,256]{2,1,0:T(8,128)(2,1)S(1)} %get-tuple-element.21), channel_id=1, source_target_pairs={{1,0},{2,1},{3,2},{4,3},{5,4},{6,5},{7,6},{8,7},{9,8},{10,9},{11,1... | collective-permute-start | bytes 393224 | tf_op jit(solution)/shard_map/ppermute | solution.py:17
  12.8 4.3 %collective-permute-start.1 = (bf16[2,128,256]{2,1,0:T(8,128)(2,1)}, bf16[2,128,256]{2,1,0:T(8,128)(2,1)S(1)}, u32[]{:S(2)}, u32[]{:S(2)}) collective-permute-start(bf16[2,128,256]{2,1,0:T(8,128)(2,1)} %get-tuple-element.22), channel_id=1, source_target_pairs={{0,2},{1,3},{2,4},{3,5},{4,6},{5,7},{6,8},{7,9},{8,10},{9,11},{10,... | collective-permute-start | bytes 393224 | tf_op jit(solution)/shard_map/ppermute | solution.py:17
  17.1 1.9 %collective-permute-start = (bf16[2,128,256]{2,1,0:T(8,128)(2,1)}, bf16[2,128,256]{2,1,0:T(8,128)(2,1)S(1)}, u32[]{:S(2)}, u32[]{:S(2)}) collective-permute-start(bf16[2,128,256]{2,1,0:T(8,128)(2,1)} %get-tuple-element.23), channel_id=1, source_target_pairs={{0,1},{1,2},{2,3},{3,4},{4,5},{5,6},{6,7},{7,8},{8,9},{9,10},{10,1... | collective-permute-start | bytes 393224 | tf_op jit(solution)/shard_map/ppermute | solution.py:17
  20.4 1.7 %collective-permute-done = bf16[2,128,256]{2,1,0:T(8,128)(2,1)S(1)} collective-permute-done((bf16[2,128,256]{2,1,0:T(8,128)(2,1)}, bf16[2,128,256]{2,1,0:T(8,128)(2,1)S(1)}, u32[]{:S(2)}, u32[]{:S(2)}) %collective-permute-start) | collective-permute-done | bytes 131104 | tf_op jit(solution)/shard_map/ppermute | solution.py:17
  24.8 1.3 collective-permute-start.7
  26.1 1.9 %collective-permute-start.6 = (bf16[2,128,256]{2,1,0:T(8,128)(2,1)S(1)}, bf16[2,128,256]{2,1,0:T(8,128)(2,1)S(1)}, u32[]{:S(2)}, u32[]{:S(2)}) collective-permute-start(bf16[2,128,256]{2,1,0:T(8,128)(2,1)S(1)} %get-tuple-element.17), channel_id=1, source_target_pairs={{1,0},{2,1},{3,2},{4,3},{5,4},{6,5},{7,6},{8,7},{9,8},{10,9},{11,1... | collective-permute-start | bytes 393224 | tf_op jit(solution)/shard_map/ppermute | solution.py:17
  28.0 5.0 %collective-permute-start.5 = (bf16[2,128,256]{2,1,0:T(8,128)(2,1)S(1)}, bf16[2,128,256]{2,1,0:T(8,128)(2,1)S(1)}, u32[]{:S(2)}, u32[]{:S(2)}) collective-permute-start(bf16[2,128,256]{2,1,0:T(8,128)(2,1)S(1)} %get-tuple-element.18), channel_id=1, source_target_pairs={{0,2},{1,3},{2,4},{3,5},{4,6},{5,7},{6,8},{7,9},{8,10},{9,11},{10,... | collective-permute-start | bytes 393224 | tf_op jit(solution)/shard_map/ppermute | solution.py:17
  33.0 3.9 %collective-permute-start.4 = (bf16[2,128,256]{2,1,0:T(8,128)(2,1)S(1)}, bf16[2,128,256]{2,1,0:T(8,128)(2,1)S(1)}, u32[]{:S(2)}, u32[]{:S(2)}) collective-permute-start(bf16[2,128,256]{2,1,0:T(8,128)(2,1)S(1)} %get-tuple-element.19), channel_id=1, source_target_pairs={{0,1},{1,2},{2,3},{3,4},{4,5},{5,6},{6,7},{7,8},{8,9},{9,10},{10,1... | collective-permute-start | bytes 393224 | tf_op jit(solution)/shard_map/ppermute | solution.py:17
  37.2 1.7 %collective-permute-done.4 = bf16[2,128,256]{2,1,0:T(8,128)(2,1)S(1)} collective-permute-done((bf16[2,128,256]{2,1,0:T(8,128)(2,1)S(1)}, bf16[2,128,256]{2,1,0:T(8,128)(2,1)S(1)}, u32[]{:S(2)}, u32[]{:S(2)}) %collective-permute-start.4) | collective-permute-done | bytes 131104 | tf_op jit(solution)/shard_map/ppermute | solution.py:17
  41.3 10.6 %all-to-all-start.1 = ((f32[32,8,2,256]{3,1,2,0:T(8,128)}), f32[32,8,2,256]{3,1,2,0:T(8,128)}, u32[]{:S(2)}, u32[]{:S(2)}) async-start(f32[32,8,2,256]{3,1,2,0:T(8,128)} %pad_maximum_fusion.1), calls=%async_computation.1 | async-start | bytes 1048576 | tf_op jit(solution)/shard_map/all_to_all | solution.py:143
  51.9 1.6 %fusion.62 = (bf16[2,768,256]{2,1,0:T(8,128)(2,1)S(1)}, f32[2,768,256]{2,1,0:T(8,128)S(1)}) fusion(bf16[256,768,1]{1,0,2:T(8,128)(2,1)S(1)} %reshape.58, bf16[2,256,256]{2,1,0:T(8,128)(2,1)S(1)} %multiply_convert_fusion, bf16[256,256]{1,0:T(8,128)(2,1)} %param.19), kind=kOutput, calls=%fused_computation.118 | convolution fusion | flops 268959744 | bytes 3145728 | tf_op jit(solution)/shard_map/nm,snd->smd/dot_general | solution.py:35
  53.5 2.4 %collective-permute-start.8 = (bf16[2,128,256]{2,1,0:T(8,128)(2,1)S(1)}, bf16[2,128,256]{2,1,0:T(8,128)(2,1)S(1)}, u32[]{:S(2)}, u32[]{:S(2)}) collective-permute-start(bf16[2,128,256]{2,1,0:T(8,128)(2,1)S(1)} %get-tuple-element.12), channel_id=1, source_target_pairs={{1,0},{2,1},{3,2},{4,3},{5,4},{6,5},{7,6},{8,7},{9,8},{10,9},{11,1... | collective-permute-start | bytes 393224 | tf_op jit(solution)/shard_map/ppermute | solution.py:17
  55.9 3.3 %collective-permute-start.11 = (bf16[2,128,256]{2,1,0:T(8,128)(2,1)S(1)}, bf16[2,128,256]{2,1,0:T(8,128)(2,1)S(1)}, u32[]{:S(2)}, u32[]{:S(2)}) collective-permute-start(bf16[2,128,256]{2,1,0:T(8,128)(2,1)S(1)} %get-tuple-element.13), channel_id=1, source_target_pairs={{0,2},{1,3},{2,4},{3,5},{4,6},{5,7},{6,8},{7,9},{8,10},{9,11},{10,... | collective-permute-start | bytes 393224 | tf_op jit(solution)/shard_map/ppermute | solution.py:17
  59.2 3.5 %collective-permute-start.10 = (bf16[2,128,256]{2,1,0:T(8,128)(2,1)S(1)}, bf16[2,128,256]{2,1,0:T(8,128)(2,1)S(1)}, u32[]{:S(2)}, u32[]{:S(2)}) collective-permute-start(bf16[2,128,256]{2,1,0:T(8,128)(2,1)S(1)} %get-tuple-element.14), channel_id=1, source_target_pairs={{0,1},{1,2},{2,3},{3,4},{4,5},{5,6},{6,7},{7,8},{8,9},{9,10},{10,1... | collective-permute-start | bytes 393224 | tf_op jit(solution)/shard_map/ppermute | solution.py:17
  62.8 1.3 collective-permute-start.9
  64.1 1.2 convolution_add_fusion.1
  65.3 7.6 %collective-permute-done.9 = bf16[2,128,256]{2,1,0:T(8,128)(2,1)S(1)} collective-permute-done((bf16[2,128,256]{2,1,0:T(8,128)(2,1)S(1)}, bf16[2,128,256]{2,1,0:T(8,128)(2,1)S(1)}, u32[]{:S(2)}, u32[]{:S(2)}) %collective-permute-start.9) | collective-permute-done | bytes 131104 | tf_op jit(solution)/shard_map/ppermute | solution.py:17
  75.2 8.8 %all-to-all-start = ((f32[32,8,2,256]{3,1,2,0:T(8,128)}), f32[32,8,2,256]{3,1,2,0:T(8,128)}, u32[]{:S(2)}, u32[]{:S(2)}) async-start(f32[32,8,2,256]{3,1,2,0:T(8,128)} %pad_maximum_fusion), calls=%async_computation | async-start | bytes 1048576 | tf_op jit(solution)/shard_map/all_to_all | solution.py:143
  86.2 2.2 %collective-permute-start.12 = (bf16[2,128,256]{2,1,0:T(8,128)(2,1)}, bf16[2,128,256]{2,1,0:T(8,128)(2,1)S(1)}, u32[]{:S(2)}, u32[]{:S(2)}) collective-permute-start(bf16[2,128,256]{2,1,0:T(8,128)(2,1)} %get-tuple-element.8), channel_id=1, source_target_pairs={{1,0},{2,1},{3,2},{4,3},{5,4},{6,5},{7,6},{8,7},{9,8},{10,9},{11,1... | collective-permute-start | bytes 393224 | tf_op jit(solution)/shard_map/ppermute | solution.py:17
  88.4 3.4 %collective-permute-start.15 = (bf16[2,128,256]{2,1,0:T(8,128)(2,1)}, bf16[2,128,256]{2,1,0:T(8,128)(2,1)S(1)}, u32[]{:S(2)}, u32[]{:S(2)}) collective-permute-start(bf16[2,128,256]{2,1,0:T(8,128)(2,1)} %get-tuple-element.9), channel_id=1, source_target_pairs={{0,2},{1,3},{2,4},{3,5},{4,6},{5,7},{6,8},{7,9},{8,10},{9,11},{10,... | collective-permute-start | bytes 393224 | tf_op jit(solution)/shard_map/ppermute | solution.py:17
  91.7 3.5 %collective-permute-start.14 = (bf16[2,128,256]{2,1,0:T(8,128)(2,1)}, bf16[2,128,256]{2,1,0:T(8,128)(2,1)S(1)}, u32[]{:S(2)}, u32[]{:S(2)}) collective-permute-start(bf16[2,128,256]{2,1,0:T(8,128)(2,1)} %get-tuple-element.10), channel_id=1, source_target_pairs={{0,1},{1,2},{2,3},{3,4},{4,5},{5,6},{6,7},{7,8},{8,9},{9,10},{10,1... | collective-permute-start | bytes 393224 | tf_op jit(solution)/shard_map/ppermute | solution.py:17
  95.3 1.3 collective-permute-start.13
  97.9 7.2 %all-to-all-done = f32[32,8,2,256]{3,1,2,0:T(8,128)} async-done(((f32[32,8,2,256]{3,1,2,0:T(8,128)}), f32[32,8,2,256]{3,1,2,0:T(8,128)}, u32[]{:S(2)}, u32[]{:S(2)}) %all-to-all-start) | async-done | bytes 524320 | tf_op jit(solution)/shard_map/all_to_all | solution.py:143
  106.2 4.7 %collective-permute-start.17 = (f32[8,4,256]{2,0,1:T(8,128)S(1)}, f32[8,4,256]{2,0,1:T(8,128)S(1)}, u32[]{:S(2)}, u32[]{:S(2)}) collective-permute-start(f32[8,4,256]{2,0,1:T(8,128)S(1)} %get-tuple-element.29), channel_id=1, source_target_pairs={{0,256},{32,288},{64,320},{96,352},{128,384},{160,416},{192,448},{... | collective-permute-start | bytes 98312 | tf_op jit(solution)/shard_map/ppermute | solution.py:113
  110.9 2.2 %collective-permute-start.16 = (f32[8,4,256]{2,0,1:T(8,128)S(1)}, f32[8,4,256]{2,0,1:T(8,128)S(1)}, u32[]{:S(2)}, u32[]{:S(2)}) collective-permute-start(f32[8,4,256]{2,0,1:T(8,128)S(1)} %get-tuple-element.29), channel_id=1, source_target_pairs={{0,128},{32,160},{64,192},{96,224},{128,256},{160,288},{192,320},{... | collective-permute-start | bytes 98312 | tf_op jit(solution)/shard_map/ppermute | solution.py:113
  113.1 4.3 %collective-permute-start.18 = (f32[8,4,256]{2,0,1:T(8,128)S(1)}, f32[8,4,256]{2,0,1:T(8,128)S(1)}, u32[]{:S(2)}, u32[]{:S(2)}) collective-permute-start(f32[8,4,256]{2,0,1:T(8,128)S(1)} %get-tuple-element.29), channel_id=1, source_target_pairs={{0,384},{32,416},{64,448},{96,480},{128,0},{160,32},{192,64},{224,... | collective-permute-start | bytes 98312 | tf_op jit(solution)/shard_map/ppermute | solution.py:113
  119.3 9.9 %collective-permute-start.21 = (f32[8,4,256]{2,0,1:T(8,128)S(1)}, f32[8,4,256]{2,0,1:T(8,128)S(1)}, u32[]{:S(2)}, u32[]{:S(2)}) collective-permute-start(f32[8,4,256]{2,0,1:T(8,128)S(1)} %fusion.92), channel_id=1, source_target_pairs={{0,96},{32,0},{64,32},{96,64},{128,224},{160,128},{192,160},{224,1... | collective-permute-start | bytes 98312 | tf_op jit(solution)/shard_map/ppermute | solution.py:113
  129.2 5.9 %collective-permute-start.20 = (f32[8,4,256]{2,0,1:T(8,128)S(1)}, f32[8,4,256]{2,0,1:T(8,128)S(1)}, u32[]{:S(2)}, u32[]{:S(2)}) collective-permute-start(f32[8,4,256]{2,0,1:T(8,128)S(1)} %fusion.92), channel_id=1, source_target_pairs={{0,64},{32,96},{64,0},{96,32},{128,192},{160,224},{192,128},{224,1... | collective-permute-start | bytes 98312 | tf_op jit(solution)/shard_map/ppermute | solution.py:113
  135.1 6.3 %collective-permute-start.19 = (f32[8,4,256]{2,0,1:T(8,128)S(1)}, f32[8,4,256]{2,0,1:T(8,128)S(1)}, u32[]{:S(2)}, u32[]{:S(2)}) collective-permute-start(f32[8,4,256]{2,0,1:T(8,128)S(1)} %fusion.92), channel_id=1, source_target_pairs={{0,32},{32,64},{64,96},{96,0},{128,160},{160,192},{192,224},{224,1... | collective-permute-start | bytes 98312 | tf_op jit(solution)/shard_map/ppermute | solution.py:113
  141.4 2.5 %collective-permute-done.20 = f32[8,4,256]{2,0,1:T(8,128)S(1)} collective-permute-done((f32[8,4,256]{2,0,1:T(8,128)S(1)}, f32[8,4,256]{2,0,1:T(8,128)S(1)}, u32[]{:S(2)}, u32[]{:S(2)}) %collective-permute-start.20) | collective-permute-done | bytes 32800 | tf_op jit(solution)/shard_map/ppermute | solution.py:113
  (107 shorter events, 17.3 us)
Async XLA Ops:
  0.6 18.7 %copy-start = (bf16[1,2,4,128,128]{4,3,2,1,0:T(8,128)(2,1)S(1)}, bf16[1,2,4,128,128]{4,3,2,1,0:T(8,128)(2,1)}, u32[]{:S(2)}) copy-start(bf16[1,2,4,128,128]{4,3,2,1,0:T(8,128)(2,1)} %param.13) | copy-start | bytes 786436
  0.6 18.4 %copy-start.1 = (bf16[2,256,256]{2,1,0:T(8,128)(2,1)S(1)}, bf16[2,256,256]{2,1,0:T(8,128)(2,1)}, u32[]{:S(2)}) copy-start(bf16[2,256,256]{2,1,0:T(8,128)(2,1)} %param.11) | copy-start | bytes 786436
  0.7 18.4 %copy-start.5 = (bf16[256,256]{1,0:T(8,128)(2,1)S(1)}, bf16[256,256]{1,0:T(8,128)(2,1)}, u32[]{:S(2)}) copy-start(bf16[256,256]{1,0:T(8,128)(2,1)} %param.16) | copy-start | bytes 393220
  0.7 18.6 %copy-start.11 = (s32[1,2,4]{2,1,0:T(2,128)S(1)}, s32[1,2,4]{2,1,0:T(2,128)}, u32[]{:S(2)}) copy-start(s32[1,2,4]{2,1,0:T(2,128)} %param.14) | copy-start | bytes 100
  2.8 19.9 %collective-permute-start.3 = (bf16[2,128,256]{2,1,0:T(8,128)(2,1)S(1)}, bf16[2,128,256]{2,1,0:T(8,128)(2,1)S(1)}, u32[]{:S(2)}, u32[]{:S(2)}) collective-permute-start(bf16[2,128,256]{2,1,0:T(8,128)(2,1)S(1)} %get-tuple-element.20), channel_id=1, source_target_pairs={{2,0},{3,1},{4,2},{5,3},{6,4},{7,5},{8,6},{9,7},{10,8},{11,9},{12,... | collective-permute-start | bytes 393224 | tf_op jit(solution)/shard_map/ppermute | solution.py:17
  4.1 18.4 %collective-permute-start.2 = (bf16[2,128,256]{2,1,0:T(8,128)(2,1)S(1)}, bf16[2,128,256]{2,1,0:T(8,128)(2,1)S(1)}, u32[]{:S(2)}, u32[]{:S(2)}) collective-permute-start(bf16[2,128,256]{2,1,0:T(8,128)(2,1)S(1)} %get-tuple-element.21), channel_id=1, source_target_pairs={{1,0},{2,1},{3,2},{4,3},{5,4},{6,5},{7,6},{8,7},{9,8},{10,9},{11,1... | collective-permute-start | bytes 393224 | tf_op jit(solution)/shard_map/ppermute | solution.py:17
  12.8 9.5 %collective-permute-start.1 = (bf16[2,128,256]{2,1,0:T(8,128)(2,1)}, bf16[2,128,256]{2,1,0:T(8,128)(2,1)S(1)}, u32[]{:S(2)}, u32[]{:S(2)}) collective-permute-start(bf16[2,128,256]{2,1,0:T(8,128)(2,1)} %get-tuple-element.22), channel_id=1, source_target_pairs={{0,2},{1,3},{2,4},{3,5},{4,6},{5,7},{6,8},{7,9},{8,10},{9,11},{10,... | collective-permute-start | bytes 393224 | tf_op jit(solution)/shard_map/ppermute | solution.py:17
  17.1 5.0 %collective-permute-start = (bf16[2,128,256]{2,1,0:T(8,128)(2,1)}, bf16[2,128,256]{2,1,0:T(8,128)(2,1)S(1)}, u32[]{:S(2)}, u32[]{:S(2)}) collective-permute-start(bf16[2,128,256]{2,1,0:T(8,128)(2,1)} %get-tuple-element.23), channel_id=1, source_target_pairs={{0,1},{1,2},{2,3},{3,4},{4,5},{5,6},{6,7},{7,8},{8,9},{9,10},{10,1... | collective-permute-start | bytes 393224 | tf_op jit(solution)/shard_map/ppermute | solution.py:17
  24.4 12.6 %copy-start.4 = (bf16[256,256]{1,0:T(8,128)(2,1)S(1)}, bf16[256,256]{1,0:T(8,128)(2,1)}, u32[]{:S(2)}) copy-start(bf16[256,256]{1,0:T(8,128)(2,1)} %param.18) | copy-start | bytes 393220
  24.8 14.2 %collective-permute-start.7 = (bf16[2,128,256]{2,1,0:T(8,128)(2,1)S(1)}, bf16[2,128,256]{2,1,0:T(8,128)(2,1)S(1)}, u32[]{:S(2)}, u32[]{:S(2)}) collective-permute-start(bf16[2,128,256]{2,1,0:T(8,128)(2,1)S(1)} %get-tuple-element.16), channel_id=1, source_target_pairs={{2,0},{3,1},{4,2},{5,3},{6,4},{7,5},{8,6},{9,7},{10,8},{11,9},{12,... | collective-permute-start | bytes 393224 | tf_op jit(solution)/shard_map/ppermute | solution.py:17
  26.1 12.9 %collective-permute-start.6 = (bf16[2,128,256]{2,1,0:T(8,128)(2,1)S(1)}, bf16[2,128,256]{2,1,0:T(8,128)(2,1)S(1)}, u32[]{:S(2)}, u32[]{:S(2)}) collective-permute-start(bf16[2,128,256]{2,1,0:T(8,128)(2,1)S(1)} %get-tuple-element.17), channel_id=1, source_target_pairs={{1,0},{2,1},{3,2},{4,3},{5,4},{6,5},{7,6},{8,7},{9,8},{10,9},{11,1... | collective-permute-start | bytes 393224 | tf_op jit(solution)/shard_map/ppermute | solution.py:17
  28.0 10.9 %collective-permute-start.5 = (bf16[2,128,256]{2,1,0:T(8,128)(2,1)S(1)}, bf16[2,128,256]{2,1,0:T(8,128)(2,1)S(1)}, u32[]{:S(2)}, u32[]{:S(2)}) collective-permute-start(bf16[2,128,256]{2,1,0:T(8,128)(2,1)S(1)} %get-tuple-element.18), channel_id=1, source_target_pairs={{0,2},{1,3},{2,4},{3,5},{4,6},{5,7},{6,8},{7,9},{8,10},{9,11},{10,... | collective-permute-start | bytes 393224 | tf_op jit(solution)/shard_map/ppermute | solution.py:17
  33.0 5.9 %collective-permute-start.4 = (bf16[2,128,256]{2,1,0:T(8,128)(2,1)S(1)}, bf16[2,128,256]{2,1,0:T(8,128)(2,1)S(1)}, u32[]{:S(2)}, u32[]{:S(2)}) collective-permute-start(bf16[2,128,256]{2,1,0:T(8,128)(2,1)S(1)} %get-tuple-element.19), channel_id=1, source_target_pairs={{0,1},{1,2},{2,3},{3,4},{4,5},{5,6},{6,7},{7,8},{8,9},{9,10},{10,1... | collective-permute-start | bytes 393224 | tf_op jit(solution)/shard_map/ppermute | solution.py:17
  41.3 34.0 %all-to-all-start.1 = ((f32[32,8,2,256]{3,1,2,0:T(8,128)}), f32[32,8,2,256]{3,1,2,0:T(8,128)}, u32[]{:S(2)}, u32[]{:S(2)}) async-start(f32[32,8,2,256]{3,1,2,0:T(8,128)} %pad_maximum_fusion.1), calls=%async_computation.1 | async-start | bytes 1048576 | tf_op jit(solution)/shard_map/all_to_all | solution.py:143
  53.5 19.4 %copy-start.14 = (f32[2,256,256]{2,1,0:T(8,128)S(1)}, f32[2,256,256]{2,1,0:T(8,128)}, u32[]{:S(2)}) copy-start(f32[2,256,256]{2,1,0:T(8,128)} %get-tuple-element.30) | copy-start | bytes 1572868
  53.5 11.7 %collective-permute-start.8 = (bf16[2,128,256]{2,1,0:T(8,128)(2,1)S(1)}, bf16[2,128,256]{2,1,0:T(8,128)(2,1)S(1)}, u32[]{:S(2)}, u32[]{:S(2)}) collective-permute-start(bf16[2,128,256]{2,1,0:T(8,128)(2,1)S(1)} %get-tuple-element.12), channel_id=1, source_target_pairs={{1,0},{2,1},{3,2},{4,3},{5,4},{6,5},{7,6},{8,7},{9,8},{10,9},{11,1... | collective-permute-start | bytes 393224 | tf_op jit(solution)/shard_map/ppermute | solution.py:17
  55.9 9.4 %collective-permute-start.11 = (bf16[2,128,256]{2,1,0:T(8,128)(2,1)S(1)}, bf16[2,128,256]{2,1,0:T(8,128)(2,1)S(1)}, u32[]{:S(2)}, u32[]{:S(2)}) collective-permute-start(bf16[2,128,256]{2,1,0:T(8,128)(2,1)S(1)} %get-tuple-element.13), channel_id=1, source_target_pairs={{0,2},{1,3},{2,4},{3,5},{4,6},{5,7},{6,8},{7,9},{8,10},{9,11},{10,... | collective-permute-start | bytes 393224 | tf_op jit(solution)/shard_map/ppermute | solution.py:17
  59.2 6.0 %collective-permute-start.10 = (bf16[2,128,256]{2,1,0:T(8,128)(2,1)S(1)}, bf16[2,128,256]{2,1,0:T(8,128)(2,1)S(1)}, u32[]{:S(2)}, u32[]{:S(2)}) collective-permute-start(bf16[2,128,256]{2,1,0:T(8,128)(2,1)S(1)} %get-tuple-element.14), channel_id=1, source_target_pairs={{0,1},{1,2},{2,3},{3,4},{4,5},{5,6},{6,7},{7,8},{8,9},{9,10},{10,1... | collective-permute-start | bytes 393224 | tf_op jit(solution)/shard_map/ppermute | solution.py:17
  62.8 10.1 %collective-permute-start.9 = (bf16[2,128,256]{2,1,0:T(8,128)(2,1)S(1)}, bf16[2,128,256]{2,1,0:T(8,128)(2,1)S(1)}, u32[]{:S(2)}, u32[]{:S(2)}) collective-permute-start(bf16[2,128,256]{2,1,0:T(8,128)(2,1)S(1)} %get-tuple-element.15), channel_id=1, source_target_pairs={{2,0},{3,1},{4,2},{5,3},{6,4},{7,5},{8,6},{9,7},{10,8},{11,9},{12,... | collective-permute-start | bytes 393224 | tf_op jit(solution)/shard_map/ppermute | solution.py:17
  75.2 29.9 %all-to-all-start = ((f32[32,8,2,256]{3,1,2,0:T(8,128)}), f32[32,8,2,256]{3,1,2,0:T(8,128)}, u32[]{:S(2)}, u32[]{:S(2)}) async-start(f32[32,8,2,256]{3,1,2,0:T(8,128)} %pad_maximum_fusion), calls=%async_computation | async-start | bytes 1048576 | tf_op jit(solution)/shard_map/all_to_all | solution.py:143
  84.7 11.9 %copy-start.6 = (bf16[256,256]{1,0:T(8,128)(2,1)S(1)}, bf16[256,256]{1,0:T(8,128)(2,1)}, u32[]{:S(2)}) copy-start(bf16[256,256]{1,0:T(8,128)(2,1)} %param.16) | copy-start | bytes 393220
  86.2 24.7 %collective-permute-start.12 = (bf16[2,128,256]{2,1,0:T(8,128)(2,1)}, bf16[2,128,256]{2,1,0:T(8,128)(2,1)S(1)}, u32[]{:S(2)}, u32[]{:S(2)}) collective-permute-start(bf16[2,128,256]{2,1,0:T(8,128)(2,1)} %get-tuple-element.8), channel_id=1, source_target_pairs={{1,0},{2,1},{3,2},{4,3},{5,4},{6,5},{7,6},{8,7},{9,8},{10,9},{11,1... | collective-permute-start | bytes 393224 | tf_op jit(solution)/shard_map/ppermute | solution.py:17
  88.4 24.7 %collective-permute-start.15 = (bf16[2,128,256]{2,1,0:T(8,128)(2,1)}, bf16[2,128,256]{2,1,0:T(8,128)(2,1)S(1)}, u32[]{:S(2)}, u32[]{:S(2)}) collective-permute-start(bf16[2,128,256]{2,1,0:T(8,128)(2,1)} %get-tuple-element.9), channel_id=1, source_target_pairs={{0,2},{1,3},{2,4},{3,5},{4,6},{5,7},{6,8},{7,9},{8,10},{9,11},{10,... | collective-permute-start | bytes 393224 | tf_op jit(solution)/shard_map/ppermute | solution.py:17
  91.7 25.7 %collective-permute-start.14 = (bf16[2,128,256]{2,1,0:T(8,128)(2,1)}, bf16[2,128,256]{2,1,0:T(8,128)(2,1)S(1)}, u32[]{:S(2)}, u32[]{:S(2)}) collective-permute-start(bf16[2,128,256]{2,1,0:T(8,128)(2,1)} %get-tuple-element.10), channel_id=1, source_target_pairs={{0,1},{1,2},{2,3},{3,4},{4,5},{5,6},{6,7},{7,8},{8,9},{9,10},{10,1... | collective-permute-start | bytes 393224 | tf_op jit(solution)/shard_map/ppermute | solution.py:17
  95.3 22.1 %collective-permute-start.13 = (bf16[2,128,256]{2,1,0:T(8,128)(2,1)}, bf16[2,128,256]{2,1,0:T(8,128)(2,1)S(1)}, u32[]{:S(2)}, u32[]{:S(2)}) collective-permute-start(bf16[2,128,256]{2,1,0:T(8,128)(2,1)} %get-tuple-element.11), channel_id=1, source_target_pairs={{2,0},{3,1},{4,2},{5,3},{6,4},{7,5},{8,6},{9,7},{10,8},{11,9},{12,... | collective-permute-start | bytes 393224 | tf_op jit(solution)/shard_map/ppermute | solution.py:17
  106.2 13.0 %copy-start.12 = (pred[4]{0:T(512)(128)(4,1)S(1)}, pred[4]{0:T(512)(128)(4,1)}, u32[]{:S(2)}) copy-start(pred[4]{0:T(512)(128)(4,1)} %compare_and_fusion.1) | copy-start | bytes 16
  106.2 12.4 %collective-permute-start.17 = (f32[8,4,256]{2,0,1:T(8,128)S(1)}, f32[8,4,256]{2,0,1:T(8,128)S(1)}, u32[]{:S(2)}, u32[]{:S(2)}) collective-permute-start(f32[8,4,256]{2,0,1:T(8,128)S(1)} %get-tuple-element.29), channel_id=1, source_target_pairs={{0,256},{32,288},{64,320},{96,352},{128,384},{160,416},{192,448},{... | collective-permute-start | bytes 98312 | tf_op jit(solution)/shard_map/ppermute | solution.py:113
  110.9 7.7 %collective-permute-start.16 = (f32[8,4,256]{2,0,1:T(8,128)S(1)}, f32[8,4,256]{2,0,1:T(8,128)S(1)}, u32[]{:S(2)}, u32[]{:S(2)}) collective-permute-start(f32[8,4,256]{2,0,1:T(8,128)S(1)} %get-tuple-element.29), channel_id=1, source_target_pairs={{0,128},{32,160},{64,192},{96,224},{128,256},{160,288},{192,320},{... | collective-permute-start | bytes 98312 | tf_op jit(solution)/shard_map/ppermute | solution.py:113
  113.1 5.5 %collective-permute-start.18 = (f32[8,4,256]{2,0,1:T(8,128)S(1)}, f32[8,4,256]{2,0,1:T(8,128)S(1)}, u32[]{:S(2)}, u32[]{:S(2)}) collective-permute-start(f32[8,4,256]{2,0,1:T(8,128)S(1)} %get-tuple-element.29), channel_id=1, source_target_pairs={{0,384},{32,416},{64,448},{96,480},{128,0},{160,32},{192,64},{224,... | collective-permute-start | bytes 98312 | tf_op jit(solution)/shard_map/ppermute | solution.py:113
  119.3 22.1 %collective-permute-start.21 = (f32[8,4,256]{2,0,1:T(8,128)S(1)}, f32[8,4,256]{2,0,1:T(8,128)S(1)}, u32[]{:S(2)}, u32[]{:S(2)}) collective-permute-start(f32[8,4,256]{2,0,1:T(8,128)S(1)} %fusion.92), channel_id=1, source_target_pairs={{0,96},{32,0},{64,32},{96,64},{128,224},{160,128},{192,160},{224,1... | collective-permute-start | bytes 98312 | tf_op jit(solution)/shard_map/ppermute | solution.py:113
  129.2 14.8 %collective-permute-start.20 = (f32[8,4,256]{2,0,1:T(8,128)S(1)}, f32[8,4,256]{2,0,1:T(8,128)S(1)}, u32[]{:S(2)}, u32[]{:S(2)}) collective-permute-start(f32[8,4,256]{2,0,1:T(8,128)S(1)} %fusion.92), channel_id=1, source_target_pairs={{0,64},{32,96},{64,0},{96,32},{128,192},{160,224},{192,128},{224,1... | collective-permute-start | bytes 98312 | tf_op jit(solution)/shard_map/ppermute | solution.py:113
  135.1 9.2 %collective-permute-start.19 = (f32[8,4,256]{2,0,1:T(8,128)S(1)}, f32[8,4,256]{2,0,1:T(8,128)S(1)}, u32[]{:S(2)}, u32[]{:S(2)}) collective-permute-start(f32[8,4,256]{2,0,1:T(8,128)S(1)} %fusion.92), channel_id=1, source_target_pairs={{0,32},{32,64},{64,96},{96,0},{128,160},{160,192},{192,224},{224,1... | collective-permute-start | bytes 98312 | tf_op jit(solution)/shard_map/ppermute | solution.py:113
  (7 other events, 27.3 us)
